TPU v7x, 32 devices: a whole 2x2x4 slice. The times are simulated.
32 devices in a mesh: gx: 8 (over z, y), gy: 4 (over x, core).
Axes of the slice: x: 2, y: 2, z: 4, core: 2. Of those that a mesh axis runs over, the one named last changes fastest.
Arguments:
- start_panel: float32 [16, 64, 128, 128], P(None, 'gx', 'gy'), may hold values from -6 to 6
- ocean_mask: int32 [64, 128, 128], P('gx', 'gy'), may hold values from 0 to 1, as said below
- conduct_x: float32 [64, 128, 128], P('gx', 'gy'), may hold values from 0.3 to 3
- conduct_y: float32 [64, 128, 128], P('gx', 'gy'), may hold values from 0.3 to 3
- conduct_z: float32 [64, 128, 128], P('gx', 'gy'), may hold values from 0.3 to 3
- diag_shift: float32 [64, 128, 128], P('gx', 'gy'), may hold values from 0.5 to 2
Outputs:
- basis_out: float32 [16, 64, 128, 128], P(None, 'gx', 'gy')
- ritz_residual: float32 [16, 64, 128, 128], P(None, 'gx', 'gy')
Inputs may be any that keep to these rules, and one draw needn't show every extreme that they name: `ocean_mask`: 1 marks an ocean cell; the share of ocean cells falls along the first dimension from about 0.9 to about 0.2.
All inputs are finite; a program needn't handle non-finite values.
Results may differ from a plain program's by a relative error of at most 0.0003.
Values sent between devices are 32-bit elements; how exact they have to be, the bound alone decides.
No kernel may reach another device: no remote copies, remote signals or barrier semaphores. Data moves between devices by JAX's collectives and lax.ppermute only.
A program may use at most 64 MiB of HBM per device.

v0:
```python
import jax
import jax.numpy as jnp
from jax import lax
from jax.sharding import PartitionSpec as P

FILTER_STEPS = 2


FILTER_CENTRE = 22.0
FILTER_HALF = 18.0
FILTER_NORM = 2.0 * (22.0 / 18.0) * (22.0 / 18.0) - 1.0


def padded_2(block, sides, width):
    for axis, dim in sides:
        count = lax.axis_size(axis)
        forward = [(i, i + 1) for i in range(count - 1)]
        backward = [(target, source) for source, target in forward]
        low = lax.ppermute(
            lax.slice_in_dim(block, block.shape[dim] - width, None, axis=dim), axis, forward
        )
        high = lax.ppermute(lax.slice_in_dim(block, 0, width, axis=dim), axis, backward)
        block = jnp.concatenate([low, block, high], axis=dim)
    return block


def stencil(values, fields):
    wet_mask = fields[0]
    along_x = fields[1]
    along_y = fields[2]
    along_z = fields[3]
    diag_term = fields[4]
    inner_wet = wet_mask[1:-1, 1:-1]
    face_x = along_x[:-1, 1:-1] * wet_mask[:-1, 1:-1] * wet_mask[1:, 1:-1]
    flow_x = face_x * (values[..., 1:, 1:-1, :] - values[..., :-1, 1:-1, :])
    face_y = along_y[1:-1, :-1] * wet_mask[1:-1, :-1] * wet_mask[1:-1, 1:]
    flow_y = face_y * (values[..., 1:-1, 1:, :] - values[..., 1:-1, :-1, :])
    centre = values[..., 1:-1, 1:-1, :]
    face_z = along_z[1:-1, 1:-1, :-1] * inner_wet[:, :, :-1] * inner_wet[:, :, 1:]
    flow_z = face_z * (centre[..., 1:] - centre[..., :-1])
    edges = [(0, 0)] * (centre.ndim - 1)
    net_z = jnp.pad(flow_z, edges + [(1, 0)]) - jnp.pad(flow_z, edges + [(0, 1)])
    net_x = flow_x[..., :-1, :, :] - flow_x[..., 1:, :, :]
    net_y = flow_y[..., :-1, :] - flow_y[..., 1:, :]
    return inner_wet * (diag_term[1:-1, 1:-1] * centre + net_x + net_y + net_z)


def operate(block, fields_one):
    padded = padded_2(block, (("gx", 1), ("gy", 2)), 1)
    return stencil(padded, fields_one)


def inner_products(left, right):
    return jnp.einsum("kc,lc->kl", left, right, precision=lax.Precision.HIGHEST)


def combine(matrix, rows):
    return jnp.einsum("kl,lc->kc", matrix, rows, precision=lax.Precision.HIGHEST)


def triangle_inverse(gram_sum, vectors):
    factor = jnp.linalg.cholesky(gram_sum)
    return lax.linalg.triangular_solve(
        factor, jnp.eye(vectors, dtype=jnp.float32), left_side=True, lower=True
    )


def on_device(start_panel, ocean_mask, conduct_x, conduct_y, conduct_z, diag_shift):
    ocean_cells = ocean_mask.astype(jnp.float32)
    fields = jnp.stack([ocean_cells, conduct_x, conduct_y, conduct_z, diag_shift])
    vectors = start_panel.shape[0]
    cell_total = (
        start_panel.shape[1]
        * start_panel.shape[2]
        * start_panel.shape[3]
        * lax.axis_size("gx")
        * lax.axis_size("gy")
    )
    field = start_panel * ocean_cells[None]
    fields_one = padded_2(fields, (("gx", 1), ("gy", 2)), 1)
    for repeat in range(FILTER_STEPS):
        middle = (operate(field, fields_one) - FILTER_CENTRE * field) / FILTER_HALF
        field = (
            2.0 * (operate(middle, fields_one) - FILTER_CENTRE * middle) / FILTER_HALF - field
        ) / FILTER_NORM
    flattened = field.reshape(vectors, -1)
    raw_images = operate(field, fields_one).reshape(vectors, -1)
    gram_sum, mixed_sum = lax.psum(
        (inner_products(flattened, flattened), inner_products(flattened, raw_images)), ("gx", "gy")
    )
    gram_sum = gram_sum / cell_total
    mixed_sum = mixed_sum / cell_total
    inverse = triangle_inverse(gram_sum, vectors)
    basis_rows = combine(inverse, flattened)
    images = combine(inverse, raw_images)
    projected = jnp.einsum(
        "ka,ab,lb->kl", inverse, mixed_sum, inverse, precision=lax.Precision.HIGHEST
    )
    residual = images - combine(projected, basis_rows)
    return (basis_rows.reshape(field.shape), residual.reshape(field.shape))


def solution(mesh):
    placed = (
        P(None, "gx", "gy", None),
        P("gx", "gy", None),
        P("gx", "gy", None),
        P("gx", "gy", None),
        P("gx", "gy", None),
        P("gx", "gy", None),
    )
    return jax.shard_map(
        on_device,
        mesh=mesh,
        in_specs=placed,
        out_specs=(P(None, "gx", "gy", None), P(None, "gx", "gy", None)),
        check_vma=False,
    )
```

profile of v0, /device:TPU:0, one launch (start us, length us, event | category | flops | bytes accessed | tf_op | source)
XLA Modules:
  0.0 212.6 jit_solution(10744945904602375748)
XLA Ops:
  5.2 4.9 %collective-permute-start = (f32[5,1,32,128]{3,2,1,0:T(8,128)S(1)}, f32[5,1,32,128]{3,2,1,0:T(8,128)S(1)}, u32[]{:S(2)}, u32[]{:S(2)}) collective-permute-start(f32[5,1,32,128]{3,2,1,0:T(8,128)S(1)} %get-tuple-element.39), channel_id=1, source_target_pairs={{0,4},{4,8},{8,12},{12,16},{16,20},{20,24},{24,28},{1,5},{5,9},{9,... | collective-permute-start | bytes 245768 | tf_op jit(solution)/shard_map/ppermute | solution.py:19
  12.4 2.9 %copy_multiply_fusion = f32[16,8,32,128]{3,0,2,1:T(8,128)S(1)} fusion(f32[16,8,32,128]{3,2,1,0:T(8,128)} %param.6, f32[8,32,128]{2,1,0:T(8,128)S(1)} %convert_element_type.16), kind=kLoop, calls=%fused_computation.105 | loop fusion | flops 524288 | bytes 4325376 | tf_op jit(solution)/shard_map/mul | solution.py:79
  19.2 4.3 %collective-permute-start.5 = (f32[16,1,32,128]{3,0,2,1:T(8,128)S(1)}, f32[16,1,32,128]{3,0,2,1:T(8,128)S(1)}, u32[]{:S(2)}, u32[]{:S(2)}) collective-permute-start(f32[16,1,32,128]{3,0,2,1:T(8,128)S(1)} %get-tuple-element.30), channel_id=1, source_target_pairs={{0,4},{4,8},{8,12},{12,16},{16,20},{20,24},{24,28},{1,5},{5,9},{9,... | collective-permute-start | bytes 786440 | tf_op jit(solution)/shard_map/ppermute | solution.py:19
  28.2 4.7 %collective-permute-done.4 = f32[16,1,32,128]{3,0,2,1:T(8,128)S(1)} collective-permute-done((f32[16,1,32,128]{3,0,2,1:T(8,128)S(1)}, f32[16,1,32,128]{3,0,2,1:T(8,128)S(1)}, u32[]{:S(2)}, u32[]{:S(2)}) %collective-permute-start.4) | collective-permute-done | bytes 262176 | tf_op jit(solution)/shard_map/ppermute | solution.py:22
  34.2 5.5 %collective-permute-start.7 = (f32[16,10,1,128]{3,0,2,1:T(8,128)S(1)}, f32[16,10,1,128]{3,0,2,1:T(8,128)S(1)}, u32[]{:S(2)}, u32[]{:S(2)}) collective-permute-start(f32[16,10,1,128]{3,0,2,1:T(8,128)S(1)} %get-tuple-element.21), channel_id=1, source_target_pairs={{0,1},{1,2},{2,3},{4,5},{5,6},{6,7},{8,9},{9,10},{10,11},{12,13},{... | collective-permute-start | bytes 245768 | tf_op jit(solution)/shard_map/ppermute | solution.py:19
  44.4 4.1 %collective-permute-start.9 = (f32[16,1,32,128]{3,0,2,1:T(8,128)S(1)}, f32[16,1,32,128]{3,0,2,1:T(8,128)S(1)}, u32[]{:S(2)}, u32[]{:S(2)}) collective-permute-start(f32[16,1,32,128]{3,0,2,1:T(8,128)S(1)} %get-tuple-element.28), channel_id=1, source_target_pairs={{0,4},{4,8},{8,12},{12,16},{16,20},{20,24},{24,28},{1,5},{5,9},{9,... | collective-permute-start | bytes 786440 | tf_op jit(solution)/shard_map/ppermute | solution.py:19
  50.5 3.0 %collective-permute-done.9 = f32[16,1,32,128]{3,0,2,1:T(8,128)S(1)} collective-permute-done((f32[16,1,32,128]{3,0,2,1:T(8,128)S(1)}, f32[16,1,32,128]{3,0,2,1:T(8,128)S(1)}, u32[]{:S(2)}, u32[]{:S(2)}) %collective-permute-start.9) | collective-permute-done | bytes 262176 | tf_op jit(solution)/shard_map/ppermute | solution.py:19
  53.5 6.0 %collective-permute-done.8 = f32[16,1,32,128]{3,0,2,1:T(8,128)S(1)} collective-permute-done((f32[16,1,32,128]{3,0,2,1:T(8,128)S(1)}, f32[16,1,32,128]{3,0,2,1:T(8,128)S(1)}, u32[]{:S(2)}, u32[]{:S(2)}) %collective-permute-start.8) | collective-permute-done | bytes 262176 | tf_op jit(solution)/shard_map/ppermute | solution.py:22
  60.8 3.4 %collective-permute-start.11 = (f32[16,10,1,128]{3,0,2,1:T(8,128)S(1)}, f32[16,10,1,128]{3,0,2,1:T(8,128)S(1)}, u32[]{:S(2)}, u32[]{:S(2)}) collective-permute-start(f32[16,10,1,128]{3,0,2,1:T(8,128)S(1)} %get-tuple-element.19), channel_id=1, source_target_pairs={{0,1},{1,2},{2,3},{4,5},{5,6},{6,7},{8,9},{9,10},{10,11},{12,13},{... | collective-permute-start | bytes 245768 | tf_op jit(solution)/shard_map/ppermute | solution.py:19
  65.4 3.3 %broadcast_multiply_fusion.1 = (f32[16,8,32,128]{3,0,2,1:T(8,128)S(1)}, f32[16,8,32,128]{3,0,2,1:T(8,128)S(1)}) fusion(f32[16,8,32,128]{3,0,2,1:T(8,128)S(1)} %get-tuple-element.11, f32[16,8,32,127]{3,0,2,1:T(8,128)S(1)} %fusion.40, f32[16,8,33,128]{3,0,2,1:T(8,128)S(1)} %fusion.12, f32[16,9,32,128]{3,0,2,1:T(8,128)S(1)} %fusion.1, ...), kind=kLoop, calls=%fused_computation.110 | loop fusion | flops 7340032 | bytes 19251200 | tf_op jit(solution)/shard_map/div | solution.py:83
  68.8 4.8 %collective-permute-start.13 = (f32[16,1,32,128]{3,0,2,1:T(8,128)S(1)}, f32[16,1,32,128]{3,0,2,1:T(8,128)S(1)}, u32[]{:S(2)}, u32[]{:S(2)}) collective-permute-start(f32[16,1,32,128]{3,0,2,1:T(8,128)S(1)} %get-tuple-element.26), channel_id=1, source_target_pairs={{0,4},{4,8},{8,12},{12,16},{16,20},{20,24},{24,28},{1,5},{5,9},{9,... | collective-permute-start | bytes 786440 | tf_op jit(solution)/shard_map/ppermute | solution.py:19
  75.5 3.0 %collective-permute-done.13 = f32[16,1,32,128]{3,0,2,1:T(8,128)S(1)} collective-permute-done((f32[16,1,32,128]{3,0,2,1:T(8,128)S(1)}, f32[16,1,32,128]{3,0,2,1:T(8,128)S(1)}, u32[]{:S(2)}, u32[]{:S(2)}) %collective-permute-start.13) | collective-permute-done | bytes 262176 | tf_op jit(solution)/shard_map/ppermute | solution.py:19
  78.5 7.5 %collective-permute-done.12 = f32[16,1,32,128]{3,0,2,1:T(8,128)S(1)} collective-permute-done((f32[16,1,32,128]{3,0,2,1:T(8,128)S(1)}, f32[16,1,32,128]{3,0,2,1:T(8,128)S(1)}, u32[]{:S(2)}, u32[]{:S(2)}) %collective-permute-start.12) | collective-permute-done | bytes 262176 | tf_op jit(solution)/shard_map/ppermute | solution.py:22
  87.3 3.3 %collective-permute-start.15 = (f32[16,10,1,128]{3,0,2,1:T(8,128)S(1)}, f32[16,10,1,128]{3,0,2,1:T(8,128)S(1)}, u32[]{:S(2)}, u32[]{:S(2)}) collective-permute-start(f32[16,10,1,128]{3,0,2,1:T(8,128)S(1)} %get-tuple-element.17), channel_id=1, source_target_pairs={{0,1},{1,2},{2,3},{4,5},{5,6},{6,7},{8,9},{9,10},{10,11},{12,13},{... | collective-permute-start | bytes 245768 | tf_op jit(solution)/shard_map/ppermute | solution.py:19
  93.3 4.9 %collective-permute-start.17 = (f32[16,1,32,128]{3,0,2,1:T(8,128)S(1)}, f32[16,1,32,128]{3,0,2,1:T(8,128)S(1)}, u32[]{:S(2)}, u32[]{:S(2)}) collective-permute-start(f32[16,1,32,128]{3,0,2,1:T(8,128)S(1)} %get-tuple-element.24), channel_id=1, source_target_pairs={{0,4},{4,8},{8,12},{12,16},{16,20},{20,24},{24,28},{1,5},{5,9},{9,... | collective-permute-start | bytes 786440 | tf_op jit(solution)/shard_map/ppermute | solution.py:19
  100.2 3.4 %collective-permute-done.17 = f32[16,1,32,128]{3,0,2,1:T(8,128)S(1)} collective-permute-done((f32[16,1,32,128]{3,0,2,1:T(8,128)S(1)}, f32[16,1,32,128]{3,0,2,1:T(8,128)S(1)}, u32[]{:S(2)}, u32[]{:S(2)}) %collective-permute-start.17) | collective-permute-done | bytes 262176 | tf_op jit(solution)/shard_map/ppermute | solution.py:19
  103.6 7.0 %collective-permute-done.16 = f32[16,1,32,128]{3,0,2,1:T(8,128)S(1)} collective-permute-done((f32[16,1,32,128]{3,0,2,1:T(8,128)S(1)}, f32[16,1,32,128]{3,0,2,1:T(8,128)S(1)}, u32[]{:S(2)}, u32[]{:S(2)}) %collective-permute-start.16) | collective-permute-done | bytes 262176 | tf_op jit(solution)/shard_map/ppermute | solution.py:22
  111.9 3.5 %collective-permute-start.19 = (f32[16,10,1,128]{3,0,2,1:T(8,128)S(1)}, f32[16,10,1,128]{3,0,2,1:T(8,128)S(1)}, u32[]{:S(2)}, u32[]{:S(2)}) collective-permute-start(f32[16,10,1,128]{3,0,2,1:T(8,128)S(1)} %get-tuple-element.15), channel_id=1, source_target_pairs={{0,1},{1,2},{2,3},{4,5},{5,6},{6,7},{8,9},{9,10},{10,11},{12,13},{... | collective-permute-start | bytes 245768 | tf_op jit(solution)/shard_map/ppermute | solution.py:19
  118.9 2.9 %convolution_bitcast_fusion.1 = f32[16,16]{0,1:T(8,128)S(1)} fusion(f32[16,8,32,128]{3,0,2,1:T(8,128)S(1)} %get-tuple-element.5), kind=kOutput, calls=%fused_computation.108 | convolution fusion | flops 101187584 | bytes 2098176 | tf_op jit(solution)/shard_map/kc,lc->kl/dot_general | solution.py:54
  121.8 4.9 %collective-permute-start.21 = (f32[16,1,32,128]{3,0,2,1:T(8,128)S(1)}, f32[16,1,32,128]{3,0,2,1:T(8,128)S(1)}, u32[]{:S(2)}, u32[]{:S(2)}) collective-permute-start(f32[16,1,32,128]{3,0,2,1:T(8,128)S(1)} %get-tuple-element.22), channel_id=1, source_target_pairs={{0,4},{4,8},{8,12},{12,16},{16,20},{20,24},{24,28},{1,5},{5,9},{9,... | collective-permute-start | bytes 786440 | tf_op jit(solution)/shard_map/ppermute | solution.py:19
  128.6 3.4 %collective-permute-done.21 = f32[16,1,32,128]{3,0,2,1:T(8,128)S(1)} collective-permute-done((f32[16,1,32,128]{3,0,2,1:T(8,128)S(1)}, f32[16,1,32,128]{3,0,2,1:T(8,128)S(1)}, u32[]{:S(2)}, u32[]{:S(2)}) %collective-permute-start.21) | collective-permute-done | bytes 262176 | tf_op jit(solution)/shard_map/ppermute | solution.py:19
  132.1 7.0 %collective-permute-done.20 = f32[16,1,32,128]{3,0,2,1:T(8,128)S(1)} collective-permute-done((f32[16,1,32,128]{3,0,2,1:T(8,128)S(1)}, f32[16,1,32,128]{3,0,2,1:T(8,128)S(1)}, u32[]{:S(2)}, u32[]{:S(2)}) %collective-permute-start.20) | collective-permute-done | bytes 262176 | tf_op jit(solution)/shard_map/ppermute | solution.py:22
  140.3 3.3 %collective-permute-start.23 = (f32[16,10,1,128]{3,0,2,1:T(8,128)S(1)}, f32[16,10,1,128]{3,0,2,1:T(8,128)S(1)}, u32[]{:S(2)}, u32[]{:S(2)}) collective-permute-start(f32[16,10,1,128]{3,0,2,1:T(8,128)S(1)} %get-tuple-element.13), channel_id=1, source_target_pairs={{0,1},{1,2},{2,3},{4,5},{5,6},{6,7},{8,9},{9,10},{10,11},{12,13},{... | collective-permute-start | bytes 245768 | tf_op jit(solution)/shard_map/ppermute | solution.py:19
  150.6 46.2 %all-reduce.10 = (f32[16,16]{0,1:T(8,128)S(1)}, f32[16,16]{0,1:T(8,128)S(1)}) all-reduce(f32[16,16]{0,1:T(8,128)S(1)} %convolution_bitcast_fusion.1, f32[16,16]{0,1:T(8,128)S(1)} %convolution_bitcast_fusion), channel_id=1, replica_groups=mesh['gx'=8,'gy'=4] {'gx','gy'}, use_global_device_ids=true, to_apply=%region_0.1 | all-reduce | flops 512 | bytes 4096 | tf_op jit(solution)/shard_map/psum | solution.py:88
  (95 shorter events, 64.2 us)
Async XLA Ops:
  5.2 10.0 %collective-permute-start = (f32[5,1,32,128]{3,2,1,0:T(8,128)S(1)}, f32[5,1,32,128]{3,2,1,0:T(8,128)S(1)}, u32[]{:S(2)}, u32[]{:S(2)}) collective-permute-start(f32[5,1,32,128]{3,2,1,0:T(8,128)S(1)} %get-tuple-element.39), channel_id=1, source_target_pairs={{0,4},{4,8},{8,12},{12,16},{16,20},{20,24},{24,28},{1,5},{5,9},{9,... | collective-permute-start | bytes 245768 | tf_op jit(solution)/shard_map/ppermute | solution.py:19
  10.1 6.3 %collective-permute-start.1 = (f32[5,1,32,128]{3,2,1,0:T(8,128)S(1)}, f32[5,1,32,128]{3,2,1,0:T(8,128)S(1)}, u32[]{:S(2)}, u32[]{:S(2)}) collective-permute-start(f32[5,1,32,128]{3,2,1,0:T(8,128)S(1)} %get-tuple-element.40), channel_id=1, source_target_pairs={{4,0},{8,4},{12,8},{16,12},{20,16},{24,20},{28,24},{5,1},{9,5},{13... | collective-permute-start | bytes 245768 | tf_op jit(solution)/shard_map/ppermute | solution.py:22
  16.5 8.3 %collective-permute-start.2 = (f32[5,10,1,128]{3,2,1,0:T(1,128)S(1)}, f32[5,10,1,128]{3,2,1,0:T(1,128)S(1)}, u32[]{:S(2)}, u32[]{:S(2)}) collective-permute-start(f32[5,10,1,128]{3,2,1,0:T(1,128)S(1)} %get-tuple-element.37), channel_id=1, source_target_pairs={{0,1},{1,2},{2,3},{4,5},{5,6},{6,7},{8,9},{9,10},{10,11},{12,13},{... | collective-permute-start | bytes 76808 | tf_op jit(solution)/shard_map/ppermute | solution.py:19
  17.8 7.0 %collective-permute-start.3 = (f32[5,10,1,128]{3,2,1,0:T(1,128)S(1)}, f32[5,10,1,128]{3,2,1,0:T(1,128)S(1)}, u32[]{:S(2)}, u32[]{:S(2)}) collective-permute-start(f32[5,10,1,128]{3,2,1,0:T(1,128)S(1)} %get-tuple-element.38), channel_id=1, source_target_pairs={{1,0},{2,1},{3,2},{5,4},{6,5},{7,6},{9,8},{10,9},{11,10},{13,12},{... | collective-permute-start | bytes 76808 | tf_op jit(solution)/shard_map/ppermute | solution.py:22
  19.2 9.1 %collective-permute-start.5 = (f32[16,1,32,128]{3,0,2,1:T(8,128)S(1)}, f32[16,1,32,128]{3,0,2,1:T(8,128)S(1)}, u32[]{:S(2)}, u32[]{:S(2)}) collective-permute-start(f32[16,1,32,128]{3,0,2,1:T(8,128)S(1)} %get-tuple-element.30), channel_id=1, source_target_pairs={{0,4},{4,8},{8,12},{12,16},{16,20},{20,24},{24,28},{1,5},{5,9},{9,... | collective-permute-start | bytes 786440 | tf_op jit(solution)/shard_map/ppermute | solution.py:19
  23.5 9.4 %collective-permute-start.4 = (f32[16,1,32,128]{3,0,2,1:T(8,128)S(1)}, f32[16,1,32,128]{3,0,2,1:T(8,128)S(1)}, u32[]{:S(2)}, u32[]{:S(2)}) collective-permute-start(f32[16,1,32,128]{3,0,2,1:T(8,128)S(1)} %get-tuple-element.31), channel_id=1, source_target_pairs={{4,0},{8,4},{12,8},{16,12},{20,16},{24,20},{28,24},{5,1},{9,5},{13... | collective-permute-start | bytes 786440 | tf_op jit(solution)/shard_map/ppermute | solution.py:22
  32.9 7.2 %collective-permute-start.6 = (f32[16,10,1,128]{3,0,2,1:T(8,128)S(1)}, f32[16,10,1,128]{3,0,2,1:T(8,128)S(1)}, u32[]{:S(2)}, u32[]{:S(2)}) collective-permute-start(f32[16,10,1,128]{3,0,2,1:T(8,128)S(1)} %get-tuple-element.20), channel_id=1, source_target_pairs={{1,0},{2,1},{3,2},{5,4},{6,5},{7,6},{9,8},{10,9},{11,10},{13,12},{... | collective-permute-start | bytes 245768 | tf_op jit(solution)/shard_map/ppermute | solution.py:22
  34.2 6.4 %collective-permute-start.7 = (f32[16,10,1,128]{3,0,2,1:T(8,128)S(1)}, f32[16,10,1,128]{3,0,2,1:T(8,128)S(1)}, u32[]{:S(2)}, u32[]{:S(2)}) collective-permute-start(f32[16,10,1,128]{3,0,2,1:T(8,128)S(1)} %get-tuple-element.21), channel_id=1, source_target_pairs={{0,1},{1,2},{2,3},{4,5},{5,6},{6,7},{8,9},{9,10},{10,11},{12,13},{... | collective-permute-start | bytes 245768 | tf_op jit(solution)/shard_map/ppermute | solution.py:19
  44.4 9.1 %collective-permute-start.9 = (f32[16,1,32,128]{3,0,2,1:T(8,128)S(1)}, f32[16,1,32,128]{3,0,2,1:T(8,128)S(1)}, u32[]{:S(2)}, u32[]{:S(2)}) collective-permute-start(f32[16,1,32,128]{3,0,2,1:T(8,128)S(1)} %get-tuple-element.28), channel_id=1, source_target_pairs={{0,4},{4,8},{8,12},{12,16},{16,20},{20,24},{24,28},{1,5},{5,9},{9,... | collective-permute-start | bytes 786440 | tf_op jit(solution)/shard_map/ppermute | solution.py:19
  48.5 11.0 %collective-permute-start.8 = (f32[16,1,32,128]{3,0,2,1:T(8,128)S(1)}, f32[16,1,32,128]{3,0,2,1:T(8,128)S(1)}, u32[]{:S(2)}, u32[]{:S(2)}) collective-permute-start(f32[16,1,32,128]{3,0,2,1:T(8,128)S(1)} %get-tuple-element.29), channel_id=1, source_target_pairs={{4,0},{8,4},{12,8},{16,12},{20,16},{24,20},{28,24},{5,1},{9,5},{13... | collective-permute-start | bytes 786440 | tf_op jit(solution)/shard_map/ppermute | solution.py:22
  59.5 5.0 %collective-permute-start.10 = (f32[16,10,1,128]{3,0,2,1:T(8,128)S(1)}, f32[16,10,1,128]{3,0,2,1:T(8,128)S(1)}, u32[]{:S(2)}, u32[]{:S(2)}) collective-permute-start(f32[16,10,1,128]{3,0,2,1:T(8,128)S(1)} %get-tuple-element.18), channel_id=1, source_target_pairs={{1,0},{2,1},{3,2},{5,4},{6,5},{7,6},{9,8},{10,9},{11,10},{13,12},{... | collective-permute-start | bytes 245768 | tf_op jit(solution)/shard_map/ppermute | solution.py:22
  60.8 4.3 %collective-permute-start.11 = (f32[16,10,1,128]{3,0,2,1:T(8,128)S(1)}, f32[16,10,1,128]{3,0,2,1:T(8,128)S(1)}, u32[]{:S(2)}, u32[]{:S(2)}) collective-permute-start(f32[16,10,1,128]{3,0,2,1:T(8,128)S(1)} %get-tuple-element.19), channel_id=1, source_target_pairs={{0,1},{1,2},{2,3},{4,5},{5,6},{6,7},{8,9},{9,10},{10,11},{12,13},{... | collective-permute-start | bytes 245768 | tf_op jit(solution)/shard_map/ppermute | solution.py:19
  68.8 9.8 %collective-permute-start.13 = (f32[16,1,32,128]{3,0,2,1:T(8,128)S(1)}, f32[16,1,32,128]{3,0,2,1:T(8,128)S(1)}, u32[]{:S(2)}, u32[]{:S(2)}) collective-permute-start(f32[16,1,32,128]{3,0,2,1:T(8,128)S(1)} %get-tuple-element.26), channel_id=1, source_target_pairs={{0,4},{4,8},{8,12},{12,16},{16,20},{20,24},{24,28},{1,5},{5,9},{9,... | collective-permute-start | bytes 786440 | tf_op jit(solution)/shard_map/ppermute | solution.py:19
  73.6 12.4 %collective-permute-start.12 = (f32[16,1,32,128]{3,0,2,1:T(8,128)S(1)}, f32[16,1,32,128]{3,0,2,1:T(8,128)S(1)}, u32[]{:S(2)}, u32[]{:S(2)}) collective-permute-start(f32[16,1,32,128]{3,0,2,1:T(8,128)S(1)} %get-tuple-element.27), channel_id=1, source_target_pairs={{4,0},{8,4},{12,8},{16,12},{20,16},{24,20},{28,24},{5,1},{9,5},{13... | collective-permute-start | bytes 786440 | tf_op jit(solution)/shard_map/ppermute | solution.py:22
  86.0 4.9 %collective-permute-start.14 = (f32[16,10,1,128]{3,0,2,1:T(8,128)S(1)}, f32[16,10,1,128]{3,0,2,1:T(8,128)S(1)}, u32[]{:S(2)}, u32[]{:S(2)}) collective-permute-start(f32[16,10,1,128]{3,0,2,1:T(8,128)S(1)} %get-tuple-element.16), channel_id=1, source_target_pairs={{1,0},{2,1},{3,2},{5,4},{6,5},{7,6},{9,8},{10,9},{11,10},{13,12},{... | collective-permute-start | bytes 245768 | tf_op jit(solution)/shard_map/ppermute | solution.py:22
  87.3 4.2 %collective-permute-start.15 = (f32[16,10,1,128]{3,0,2,1:T(8,128)S(1)}, f32[16,10,1,128]{3,0,2,1:T(8,128)S(1)}, u32[]{:S(2)}, u32[]{:S(2)}) collective-permute-start(f32[16,10,1,128]{3,0,2,1:T(8,128)S(1)} %get-tuple-element.17), channel_id=1, source_target_pairs={{0,1},{1,2},{2,3},{4,5},{5,6},{6,7},{8,9},{9,10},{10,11},{12,13},{... | collective-permute-start | bytes 245768 | tf_op jit(solution)/shard_map/ppermute | solution.py:19
  93.3 10.3 %collective-permute-start.17 = (f32[16,1,32,128]{3,0,2,1:T(8,128)S(1)}, f32[16,1,32,128]{3,0,2,1:T(8,128)S(1)}, u32[]{:S(2)}, u32[]{:S(2)}) collective-permute-start(f32[16,1,32,128]{3,0,2,1:T(8,128)S(1)} %get-tuple-element.24), channel_id=1, source_target_pairs={{0,4},{4,8},{8,12},{12,16},{16,20},{20,24},{24,28},{1,5},{5,9},{9,... | collective-permute-start | bytes 786440 | tf_op jit(solution)/shard_map/ppermute | solution.py:19
  98.2 12.3 %collective-permute-start.16 = (f32[16,1,32,128]{3,0,2,1:T(8,128)S(1)}, f32[16,1,32,128]{3,0,2,1:T(8,128)S(1)}, u32[]{:S(2)}, u32[]{:S(2)}) collective-permute-start(f32[16,1,32,128]{3,0,2,1:T(8,128)S(1)} %get-tuple-element.25), channel_id=1, source_target_pairs={{4,0},{8,4},{12,8},{16,12},{20,16},{24,20},{28,24},{5,1},{9,5},{13... | collective-permute-start | bytes 786440 | tf_op jit(solution)/shard_map/ppermute | solution.py:22
  110.6 5.2 %collective-permute-start.18 = (f32[16,10,1,128]{3,0,2,1:T(8,128)S(1)}, f32[16,10,1,128]{3,0,2,1:T(8,128)S(1)}, u32[]{:S(2)}, u32[]{:S(2)}) collective-permute-start(f32[16,10,1,128]{3,0,2,1:T(8,128)S(1)} %get-tuple-element.14), channel_id=1, source_target_pairs={{1,0},{2,1},{3,2},{5,4},{6,5},{7,6},{9,8},{10,9},{11,10},{13,12},{... | collective-permute-start | bytes 245768 | tf_op jit(solution)/shard_map/ppermute | solution.py:22
  111.9 4.2 %collective-permute-start.19 = (f32[16,10,1,128]{3,0,2,1:T(8,128)S(1)}, f32[16,10,1,128]{3,0,2,1:T(8,128)S(1)}, u32[]{:S(2)}, u32[]{:S(2)}) collective-permute-start(f32[16,10,1,128]{3,0,2,1:T(8,128)S(1)} %get-tuple-element.15), channel_id=1, source_target_pairs={{0,1},{1,2},{2,3},{4,5},{5,6},{6,7},{8,9},{9,10},{10,11},{12,13},{... | collective-permute-start | bytes 245768 | tf_op jit(solution)/shard_map/ppermute | solution.py:19
  121.8 10.3 %collective-permute-start.21 = (f32[16,1,32,128]{3,0,2,1:T(8,128)S(1)}, f32[16,1,32,128]{3,0,2,1:T(8,128)S(1)}, u32[]{:S(2)}, u32[]{:S(2)}) collective-permute-start(f32[16,1,32,128]{3,0,2,1:T(8,128)S(1)} %get-tuple-element.22), channel_id=1, source_target_pairs={{0,4},{4,8},{8,12},{12,16},{16,20},{20,24},{24,28},{1,5},{5,9},{9,... | collective-permute-start | bytes 786440 | tf_op jit(solution)/shard_map/ppermute | solution.py:19
  126.7 12.3 %collective-permute-start.20 = (f32[16,1,32,128]{3,0,2,1:T(8,128)S(1)}, f32[16,1,32,128]{3,0,2,1:T(8,128)S(1)}, u32[]{:S(2)}, u32[]{:S(2)}) collective-permute-start(f32[16,1,32,128]{3,0,2,1:T(8,128)S(1)} %get-tuple-element.23), channel_id=1, source_target_pairs={{4,0},{8,4},{12,8},{16,12},{20,16},{24,20},{28,24},{5,1},{9,5},{13... | collective-permute-start | bytes 786440 | tf_op jit(solution)/shard_map/ppermute | solution.py:22
  139.0 4.9 %collective-permute-start.22 = (f32[16,10,1,128]{3,0,2,1:T(8,128)S(1)}, f32[16,10,1,128]{3,0,2,1:T(8,128)S(1)}, u32[]{:S(2)}, u32[]{:S(2)}) collective-permute-start(f32[16,10,1,128]{3,0,2,1:T(8,128)S(1)} %get-tuple-element.12), channel_id=1, source_target_pairs={{1,0},{2,1},{3,2},{5,4},{6,5},{7,6},{9,8},{10,9},{11,10},{13,12},{... | collective-permute-start | bytes 245768 | tf_op jit(solution)/shard_map/ppermute | solution.py:22
  140.3 4.2 %collective-permute-start.23 = (f32[16,10,1,128]{3,0,2,1:T(8,128)S(1)}, f32[16,10,1,128]{3,0,2,1:T(8,128)S(1)}, u32[]{:S(2)}, u32[]{:S(2)}) collective-permute-start(f32[16,10,1,128]{3,0,2,1:T(8,128)S(1)} %get-tuple-element.13), channel_id=1, source_target_pairs={{0,1},{1,2},{2,3},{4,5},{5,6},{6,7},{8,9},{9,10},{10,11},{12,13},{... | collective-permute-start | bytes 245768 | tf_op jit(solution)/shard_map/ppermute | solution.py:19
  (2 other events, 4.8 us)
where the time goes:
time: 214 us; the launch traced here: 213 us
  starting transfers between devices  63.7 us (30%)
  waiting for transfers between devices  51 us (24%)
  blocking collectives  46.2 us (22%)
  other arithmetic  25.8 us (12%)
  matrix products  13.8 us (6%)
  local copies, waits for them, and re-layouts  10.8 us (5%)
    ppermute x12, starting transfers between devices, padded_2(): lax.ppermute(lax.slice_in_dim(block, block.shape[dim] - width, None, axis...  48.2 us
    psum x1, blocking collectives, on_device(): lax.psum((inner_products(flattened, flattened), inner_products(flattened,...  46.2 us
    ppermute x12, waiting for transfers between devices, padded_2(): lax.ppermute(lax.slice_in_dim(block, 0, width, axis=dim), axis, backward)  33.3 us
    ppermute x12, waiting for transfers between devices, padded_2(): lax.ppermute(lax.slice_in_dim(block, block.shape[dim] - width, None, axis...  17.7 us
    ppermute x12, starting transfers between devices, padded_2(): lax.ppermute(lax.slice_in_dim(block, 0, width, axis=dim), axis, backward)  15.5 us
    dot_general x3, matrix products, combine(): jnp.einsum('kl,lc->kc', matrix, rows, precision=lax.Precision.HIGHEST)  7.62 us
    unnamed x9, local copies, waits for them, and re-layouts  6.92 us
    dot_general x2, matrix products, inner_products(): return jnp.einsum('kc,lc->kl', left, right, precision=lax.Precision.HIGHEST)  5.66 us
  transfers between devices with their start and end apart: 24, of which 16 were waited for; matrix products, arithmetic and copies ran while one was open for 4% of the time, Pallas kernels for 0%

commit v1 on v0

--- a/solution.py
+++ b/solution.py
@@ -11,17 +11,25 @@
 FILTER_NORM = 2.0 * (22.0 / 18.0) * (22.0 / 18.0) - 1.0
 
 
+def halo_pair(block, axis, dim):
+    count = lax.axis_size(axis)
+    forward = [(i, i + 1) for i in range(count - 1)]
+    backward = [(target, source) for source, target in forward]
+    low = lax.ppermute(lax.slice_in_dim(block, block.shape[dim] - 1, None, axis=dim), axis, forward)
+    high = lax.ppermute(lax.slice_in_dim(block, 0, 1, axis=dim), axis, backward)
+    return low, high
+
+
 def padded_2(block, sides, width):
-    for axis, dim in sides:
-        count = lax.axis_size(axis)
-        forward = [(i, i + 1) for i in range(count - 1)]
-        backward = [(target, source) for source, target in forward]
-        low = lax.ppermute(
-            lax.slice_in_dim(block, block.shape[dim] - width, None, axis=dim), axis, forward
-        )
-        high = lax.ppermute(lax.slice_in_dim(block, 0, width, axis=dim), axis, backward)
-        block = jnp.concatenate([low, block, high], axis=dim)
-    return block
+    (axis_a, dim_a), (axis_b, dim_b) = sides
+    low_a, high_a = halo_pair(block, axis_a, dim_a)
+    low_b, high_b = halo_pair(block, axis_b, dim_b)
+    block = jnp.concatenate([low_a, block, high_a], axis=dim_a)
+    edge = [(0, 0)] * block.ndim
+    edge[dim_a] = (1, 1)
+    low_b = jnp.pad(low_b, edge)
+    high_b = jnp.pad(high_b, edge)
+    return jnp.concatenate([low_b, block, high_b], axis=dim_b)
 
 
 def stencil(values, fields):
@@ -48,6 +56,18 @@
 def operate(block, fields_one):
     padded = padded_2(block, (("gx", 1), ("gy", 2)), 1)
     return stencil(padded, fields_one)
+
+
+def reduce_all(value):
+    for axis in ("gy", "gx"):
+        count = lax.axis_size(axis)
+        assert count & (count - 1) == 0
+        step = 1
+        while step < count:
+            pairs = [(i, i ^ step) for i in range(count)]
+            value = value + lax.ppermute(value, axis, pairs)
+            step *= 2
+    return value
 
 
 def inner_products(left, right):
@@ -85,11 +105,11 @@
         ) / FILTER_NORM
     flattened = field.reshape(vectors, -1)
     raw_images = operate(field, fields_one).reshape(vectors, -1)
-    gram_sum, mixed_sum = lax.psum(
-        (inner_products(flattened, flattened), inner_products(flattened, raw_images)), ("gx", "gy")
+    sums = reduce_all(
+        jnp.stack([inner_products(flattened, flattened), inner_products(flattened, raw_images)])
     )
-    gram_sum = gram_sum / cell_total
-    mixed_sum = mixed_sum / cell_total
+    gram_sum = sums[0] / cell_total
+    mixed_sum = sums[1] / cell_total
     inverse = triangle_inverse(gram_sum, vectors)
     basis_rows = combine(inverse, flattened)
     images = combine(inverse, raw_images)

time: 214 us -> 190 us (0.89)
  blocking collectives: 46.2 us -> 0 us
  starting transfers between devices: 63.7 us -> 75 us
  waiting for transfers between devices: 51 us -> 60 us
  matrix products: 13.8 us -> 16.6 us
    psum x1 -> x0, blocking collectives: 46.2 us -> none  [on_device(): lax.psum((inner_products(flattened, flattened), inner_products(flattened,...]
    ppermute x24 -> x29, starting transfers between devices: 63.7 us -> 75 us  [the longest x12 48.7 us: halo_pair(): lax.ppermute(lax.slice_in_dim(block, block.shape[dim] - 1, None, axis=dim...]
    ppermute x24 -> x29, waiting for transfers between devices: 51 us -> 60 us  [the longest x12 30 us: halo_pair(): high = lax.ppermute(lax.slice_in_dim(block, 0, 1, axis=dim), axis, backward)]
    mul x5, other arithmetic: 1.42 us -> 4.35 us  [stencil(): flow_y = face_y * (values[..., 1:-1, 1:, :] - values[..., 1:-1, :-1, :])]
    dot_general x2, matrix products: 5.66 us -> 8.14 us  [inner_products(): return jnp.einsum('kc,lc->kl', left, right, precision=lax.Precision.HIGHEST)]
    unnamed x9 -> x13, local copies, waits for them, and re-layouts: 6.92 us -> 7.67 us
  transfers between devices with their start and end apart: 24 -> 29, of which waited for: 16 -> 15; matrix products, arithmetic and copies ran while one was open for 4% -> 4% of each run, Pallas kernels for 0% -> 0%
where the time goes in v1:
time: 190 us; the launch traced here: 189 us
  starting transfers between devices  75 us (39%)
  waiting for transfers between devices  60 us (32%)
  other arithmetic  26.6 us (14%)
  matrix products  16.6 us (9%)
  local copies, waits for them, and re-layouts  9.45 us (5%)
    ppermute x12, starting transfers between devices, halo_pair(): lax.ppermute(lax.slice_in_dim(block, block.shape[dim] - 1, None, axis=dim...  48.7 us
    ppermute x12, waiting for transfers between devices, halo_pair(): high = lax.ppermute(lax.slice_in_dim(block, 0, 1, axis=dim), axis, backward)  30 us
    ppermute x12, waiting for transfers between devices, halo_pair(): lax.ppermute(lax.slice_in_dim(block, block.shape[dim] - 1, None, axis=dim...  20.1 us
    ppermute x12, starting transfers between devices, halo_pair(): high = lax.ppermute(lax.slice_in_dim(block, 0, 1, axis=dim), axis, backward)  15.7 us
    ppermute x5, starting transfers between devices, reduce_all(): value = value + lax.ppermute(value, axis, pairs)  10.7 us
    ppermute x5, waiting for transfers between devices, reduce_all(): value = value + lax.ppermute(value, axis, pairs)  9.94 us
    dot_general x2, matrix products, inner_products(): return jnp.einsum('kc,lc->kl', left, right, precision=lax.Precision.HIGHEST)  8.14 us
    dot_general x3, matrix products, combine(): jnp.einsum('kl,lc->kc', matrix, rows, precision=lax.Precision.HIGHEST)  7.9 us
  transfers between devices with their start and end apart: 29, of which 15 were waited for; matrix products, arithmetic and copies ran while one was open for 4% of the time, Pallas kernels for 0%

profile of v1, /device:TPU:0, one launch (start us, length us, event | category | flops | bytes accessed | tf_op | source)
XLA Modules:
  0.0 188.9 jit_solution(9087598215964062870)
XLA Ops:
  9.0 4.3 %collective-permute-start.1 = (f32[5,1,32,128]{3,2,1,0:T(8,128)S(1)}, f32[5,1,32,128]{3,2,1,0:T(8,128)S(1)}, u32[]{:S(2)}, u32[]{:S(2)}) collective-permute-start(f32[5,1,32,128]{3,2,1,0:T(8,128)S(1)} %get-tuple-element.35), channel_id=1, source_target_pairs={{0,4},{4,8},{8,12},{12,16},{16,20},{20,24},{24,28},{1,5},{5,9},{9,... | collective-permute-start | bytes 245768 | tf_op jit(solution)/shard_map/ppermute | solution.py:18
  18.7 4.7 %collective-permute-start.7 = (f32[16,8,1,128]{3,2,1,0:T(1,128)S(1)}, f32[16,8,1,128]{3,2,1,0:T(1,128)S(1)}, u32[]{:S(2)}, u32[]{:S(2)}) collective-permute-start(f32[16,8,1,128]{3,2,1,0:T(1,128)S(1)} %get-tuple-element.27), channel_id=1, source_target_pairs={{0,1},{1,2},{2,3},{4,5},{5,6},{6,7},{8,9},{9,10},{10,11},{12,13},{... | collective-permute-start | bytes 196616 | tf_op jit(solution)/shard_map/ppermute | solution.py:18
  23.4 4.3 %collective-permute-start.5 = (f32[16,1,32,128]{3,2,1,0:T(8,128)S(1)}, f32[16,1,32,128]{3,2,1,0:T(8,128)S(1)}, u32[]{:S(2)}, u32[]{:S(2)}) collective-permute-start(f32[16,1,32,128]{3,2,1,0:T(8,128)S(1)} %get-tuple-element.28), channel_id=1, source_target_pairs={{0,4},{4,8},{8,12},{12,16},{16,20},{20,24},{24,28},{1,5},{5,9},{9,... | collective-permute-start | bytes 786440 | tf_op jit(solution)/shard_map/ppermute | solution.py:18
  33.0 4.8 %collective-permute-done.4 = f32[16,1,32,128]{3,2,1,0:T(8,128)S(1)} collective-permute-done((f32[16,1,32,128]{3,2,1,0:T(8,128)S(1)}, f32[16,1,32,128]{3,2,1,0:T(8,128)S(1)}, u32[]{:S(2)}, u32[]{:S(2)}) %collective-permute-start.4) | collective-permute-done | bytes 262176 | tf_op jit(solution)/shard_map/ppermute | solution.py:19
  42.7 4.8 %collective-permute-start.11 = (f32[16,8,1,128]{3,2,1,0:T(1,128)S(1)}, f32[16,8,1,128]{3,2,1,0:T(1,128)S(1)}, u32[]{:S(2)}, u32[]{:S(2)}) collective-permute-start(f32[16,8,1,128]{3,2,1,0:T(1,128)S(1)} %get-tuple-element.23), channel_id=1, source_target_pairs={{0,1},{1,2},{2,3},{4,5},{5,6},{6,7},{8,9},{9,10},{10,11},{12,13},{... | collective-permute-start | bytes 196616 | tf_op jit(solution)/shard_map/ppermute | solution.py:18
  47.6 4.1 %collective-permute-start.9 = (f32[16,1,32,128]{3,2,1,0:T(8,128)S(1)}, f32[16,1,32,128]{3,2,1,0:T(8,128)S(1)}, u32[]{:S(2)}, u32[]{:S(2)}) collective-permute-start(f32[16,1,32,128]{3,2,1,0:T(8,128)S(1)} %get-tuple-element.24), channel_id=1, source_target_pairs={{0,4},{4,8},{8,12},{12,16},{16,20},{20,24},{24,28},{1,5},{5,9},{9,... | collective-permute-start | bytes 786440 | tf_op jit(solution)/shard_map/ppermute | solution.py:18
  53.6 4.0 %collective-permute-done.9 = f32[16,1,32,128]{3,2,1,0:T(8,128)S(1)} collective-permute-done((f32[16,1,32,128]{3,2,1,0:T(8,128)S(1)}, f32[16,1,32,128]{3,2,1,0:T(8,128)S(1)}, u32[]{:S(2)}, u32[]{:S(2)}) %collective-permute-start.9) | collective-permute-done | bytes 262176 | tf_op jit(solution)/shard_map/ppermute | solution.py:18
  57.6 6.7 %collective-permute-done.8 = f32[16,1,32,128]{3,2,1,0:T(8,128)S(1)} collective-permute-done((f32[16,1,32,128]{3,2,1,0:T(8,128)S(1)}, f32[16,1,32,128]{3,2,1,0:T(8,128)S(1)}, u32[]{:S(2)}, u32[]{:S(2)}) %collective-permute-start.8) | collective-permute-done | bytes 262176 | tf_op jit(solution)/shard_map/ppermute | solution.py:19
  71.9 5.0 %collective-permute-start.13 = (f32[16,1,32,128]{3,2,1,0:T(8,128)S(1)}, f32[16,1,32,128]{3,2,1,0:T(8,128)S(1)}, u32[]{:S(2)}, u32[]{:S(2)}) collective-permute-start(f32[16,1,32,128]{3,2,1,0:T(8,128)S(1)} %get-tuple-element.20), channel_id=1, source_target_pairs={{0,4},{4,8},{8,12},{12,16},{16,20},{20,24},{24,28},{1,5},{5,9},{9,... | collective-permute-start | bytes 786440 | tf_op jit(solution)/shard_map/ppermute | solution.py:18
  78.8 4.4 %collective-permute-done.13 = f32[16,1,32,128]{3,2,1,0:T(8,128)S(1)} collective-permute-done((f32[16,1,32,128]{3,2,1,0:T(8,128)S(1)}, f32[16,1,32,128]{3,2,1,0:T(8,128)S(1)}, u32[]{:S(2)}, u32[]{:S(2)}) %collective-permute-start.13) | collective-permute-done | bytes 262176 | tf_op jit(solution)/shard_map/ppermute | solution.py:18
  83.3 6.2 %collective-permute-done.12 = f32[16,1,32,128]{3,2,1,0:T(8,128)S(1)} collective-permute-done((f32[16,1,32,128]{3,2,1,0:T(8,128)S(1)}, f32[16,1,32,128]{3,2,1,0:T(8,128)S(1)}, u32[]{:S(2)}, u32[]{:S(2)}) %collective-permute-start.12) | collective-permute-done | bytes 262176 | tf_op jit(solution)/shard_map/ppermute | solution.py:19
  97.8 5.0 %collective-permute-start.17 = (f32[16,1,32,128]{3,2,1,0:T(8,128)S(1)}, f32[16,1,32,128]{3,2,1,0:T(8,128)S(1)}, u32[]{:S(2)}, u32[]{:S(2)}) collective-permute-start(f32[16,1,32,128]{3,2,1,0:T(8,128)S(1)} %get-tuple-element.16), channel_id=1, source_target_pairs={{0,4},{4,8},{8,12},{12,16},{16,20},{20,24},{24,28},{1,5},{5,9},{9,... | collective-permute-start | bytes 786440 | tf_op jit(solution)/shard_map/ppermute | solution.py:18
  105.0 4.3 %collective-permute-done.17 = f32[16,1,32,128]{3,2,1,0:T(8,128)S(1)} collective-permute-done((f32[16,1,32,128]{3,2,1,0:T(8,128)S(1)}, f32[16,1,32,128]{3,2,1,0:T(8,128)S(1)}, u32[]{:S(2)}, u32[]{:S(2)}) %collective-permute-start.17) | collective-permute-done | bytes 262176 | tf_op jit(solution)/shard_map/ppermute | solution.py:18
  109.2 6.2 %collective-permute-done.16 = f32[16,1,32,128]{3,2,1,0:T(8,128)S(1)} collective-permute-done((f32[16,1,32,128]{3,2,1,0:T(8,128)S(1)}, f32[16,1,32,128]{3,2,1,0:T(8,128)S(1)}, u32[]{:S(2)}, u32[]{:S(2)}) %collective-permute-start.16) | collective-permute-done | bytes 262176 | tf_op jit(solution)/shard_map/ppermute | solution.py:19
  119.2 3.6 %fusion.70 = f32[1,16,16]{1,2,0:T(8,128)S(1)} fusion(f32[16,8,32,128]{3,2,1,0:T(8,128)S(1)} %get-tuple-element.2), kind=kOutput, calls=%fused_computation.123 | convolution fusion | flops 100663296 | bytes 2098176 | tf_op jit(solution)/shard_map/kc,lc->kl/dot_general | solution.py:74
  127.3 5.0 %collective-permute-start.21 = (f32[16,1,32,128]{3,2,1,0:T(8,128)S(1)}, f32[16,1,32,128]{3,2,1,0:T(8,128)S(1)}, u32[]{:S(2)}, u32[]{:S(2)}) collective-permute-start(f32[16,1,32,128]{3,2,1,0:T(8,128)S(1)} %get-tuple-element.12), channel_id=1, source_target_pairs={{0,4},{4,8},{8,12},{12,16},{16,20},{20,24},{24,28},{1,5},{5,9},{9,... | collective-permute-start | bytes 786440 | tf_op jit(solution)/shard_map/ppermute | solution.py:18
  134.2 4.4 %collective-permute-done.21 = f32[16,1,32,128]{3,2,1,0:T(8,128)S(1)} collective-permute-done((f32[16,1,32,128]{3,2,1,0:T(8,128)S(1)}, f32[16,1,32,128]{3,2,1,0:T(8,128)S(1)}, u32[]{:S(2)}, u32[]{:S(2)}) %collective-permute-start.21) | collective-permute-done | bytes 262176 | tf_op jit(solution)/shard_map/ppermute | solution.py:18
  138.7 6.2 %collective-permute-done.20 = f32[16,1,32,128]{3,2,1,0:T(8,128)S(1)} collective-permute-done((f32[16,1,32,128]{3,2,1,0:T(8,128)S(1)}, f32[16,1,32,128]{3,2,1,0:T(8,128)S(1)}, u32[]{:S(2)}, u32[]{:S(2)}) %collective-permute-start.20) | collective-permute-done | bytes 262176 | tf_op jit(solution)/shard_map/ppermute | solution.py:19
  147.7 4.5 %fusion.73 = f32[1,16,16]{1,2,0:T(8,128)S(1)} fusion(f32[16,8,32,128]{3,2,1,0:T(8,128)S(1)} %fusion.34, f32[16,8,32,128]{3,2,1,0:T(8,128)S(1)} %get-tuple-element.2), kind=kOutput, calls=%fused_computation.124 | convolution fusion | flops 100663296 | bytes 4195328 | tf_op jit(solution)/shard_map/kc,lc->kl/dot_general | solution.py:74
  153.5 3.7 %collective-permute-done.25 = f32[2,16,16]{1,2,0:T(8,128)S(1)} collective-permute-done((f32[2,16,16]{1,2,0:T(8,128)S(1)}, f32[2,16,16]{1,2,0:T(8,128)S(1)}, u32[]{:S(2)}, u32[]{:S(2)}) %collective-permute-start.25) | collective-permute-done | bytes 2080 | tf_op jit(solution)/shard_map/ppermute | solution.py:68
  157.3 3.1 %collective-permute-start.26 = (f32[2,16,16]{1,2,0:T(8,128)S(1)}, f32[2,16,16]{1,2,0:T(8,128)S(1)}, u32[]{:S(2)}, u32[]{:S(2)}) collective-permute-start(f32[2,16,16]{1,2,0:T(8,128)S(1)} %fusion.113), channel_id=1, source_target_pairs={{0,4},{4,0},{8,12},{12,8},{16,20},{20,16},{24,28},{28,24},{1,5},{5... | collective-permute-start | bytes 6152 | tf_op jit(solution)/shard_map/ppermute | solution.py:68
  162.1 4.3 %collective-permute-start.27 = (f32[2,16,16]{1,2,0:T(8,128)S(1)}, f32[2,16,16]{1,2,0:T(8,128)S(1)}, u32[]{:S(2)}, u32[]{:S(2)}) collective-permute-start(f32[2,16,16]{1,2,0:T(8,128)S(1)} %add.132), channel_id=1, source_target_pairs={{0,8},{4,12},{8,0},{12,4},{16,24},{20,28},{24,16},{28,20},{1,9},{5... | collective-permute-start | bytes 6152 | tf_op jit(solution)/shard_map/ppermute | solution.py:68
  168.2 3.0 %collective-permute-start.28 = (f32[2,16,16]{1,2,0:T(8,128)S(1)}, f32[2,16,16]{1,2,0:T(8,128)S(1)}, u32[]{:S(2)}, u32[]{:S(2)}) collective-permute-start(f32[2,16,16]{1,2,0:T(8,128)S(1)} %add.133), channel_id=1, source_target_pairs={{0,16},{4,20},{8,24},{12,28},{16,0},{20,4},{24,8},{28,12},{1,17},{... | collective-permute-start | bytes 6152 | tf_op jit(solution)/shard_map/ppermute | solution.py:68
  180.4 3.1 %fusion.25 = f32[16,32768]{1,0:T(8,128)S(1)} fusion(f32[16,16]{1,0:T(8,128)S(1)} %fusion.83, f32[2,8,256,128]{3,2,1,0:T(8,128)S(1)} %bitcast.68), kind=kOutput, calls=%fused_computation.63 | convolution fusion | flops 100663296 | bytes 4195328 | tf_op jit(solution)/shard_map/kl,lc->kc/dot_general | solution.py:78
  (112 shorter events, 77.8 us)
Async XLA Ops:
  5.3 13.5 %collective-permute-start = (f32[5,8,1,128]{3,2,1,0:T(1,128)S(1)}, f32[5,8,1,128]{3,2,1,0:T(1,128)S(1)}, u32[]{:S(2)}, u32[]{:S(2)}) collective-permute-start(f32[5,8,1,128]{3,2,1,0:T(1,128)S(1)} %get-tuple-element.37), channel_id=1, source_target_pairs={{0,1},{1,2},{2,3},{4,5},{5,6},{6,7},{8,9},{9,10},{10,11},{12,13},{... | collective-permute-start | bytes 61448 | tf_op jit(solution)/shard_map/ppermute | solution.py:18
  7.6 15.8 %collective-permute-start.3 = (f32[5,8,1,128]{3,2,1,0:T(1,128)S(1)}, f32[5,8,1,128]{3,2,1,0:T(1,128)S(1)}, u32[]{:S(2)}, u32[]{:S(2)}) collective-permute-start(f32[5,8,1,128]{3,2,1,0:T(1,128)S(1)} %get-tuple-element.38), channel_id=1, source_target_pairs={{1,0},{2,1},{3,2},{5,4},{6,5},{7,6},{9,8},{10,9},{11,10},{13,12},{... | collective-permute-start | bytes 61448 | tf_op jit(solution)/shard_map/ppermute | solution.py:19
  9.0 18.8 %collective-permute-start.1 = (f32[5,1,32,128]{3,2,1,0:T(8,128)S(1)}, f32[5,1,32,128]{3,2,1,0:T(8,128)S(1)}, u32[]{:S(2)}, u32[]{:S(2)}) collective-permute-start(f32[5,1,32,128]{3,2,1,0:T(8,128)S(1)} %get-tuple-element.35), channel_id=1, source_target_pairs={{0,4},{4,8},{8,12},{12,16},{16,20},{20,24},{24,28},{1,5},{5,9},{9,... | collective-permute-start | bytes 245768 | tf_op jit(solution)/shard_map/ppermute | solution.py:18
  13.2 15.8 %collective-permute-start.2 = (f32[5,1,32,128]{3,2,1,0:T(8,128)S(1)}, f32[5,1,32,128]{3,2,1,0:T(8,128)S(1)}, u32[]{:S(2)}, u32[]{:S(2)}) collective-permute-start(f32[5,1,32,128]{3,2,1,0:T(8,128)S(1)} %get-tuple-element.36), channel_id=1, source_target_pairs={{4,0},{8,4},{12,8},{16,12},{20,16},{24,20},{28,24},{5,1},{9,5},{13... | collective-permute-start | bytes 245768 | tf_op jit(solution)/shard_map/ppermute | solution.py:19
  17.4 20.9 %collective-permute-start.6 = (f32[16,8,1,128]{3,2,1,0:T(1,128)S(1)}, f32[16,8,1,128]{3,2,1,0:T(1,128)S(1)}, u32[]{:S(2)}, u32[]{:S(2)}) collective-permute-start(f32[16,8,1,128]{3,2,1,0:T(1,128)S(1)} %get-tuple-element.26), channel_id=1, source_target_pairs={{1,0},{2,1},{3,2},{5,4},{6,5},{7,6},{9,8},{10,9},{11,10},{13,12},{... | collective-permute-start | bytes 196616 | tf_op jit(solution)/shard_map/ppermute | solution.py:19
  18.7 19.5 %collective-permute-start.7 = (f32[16,8,1,128]{3,2,1,0:T(1,128)S(1)}, f32[16,8,1,128]{3,2,1,0:T(1,128)S(1)}, u32[]{:S(2)}, u32[]{:S(2)}) collective-permute-start(f32[16,8,1,128]{3,2,1,0:T(1,128)S(1)} %get-tuple-element.27), channel_id=1, source_target_pairs={{0,1},{1,2},{2,3},{4,5},{5,6},{6,7},{8,9},{9,10},{10,11},{12,13},{... | collective-permute-start | bytes 196616 | tf_op jit(solution)/shard_map/ppermute | solution.py:18
  23.4 9.6 %collective-permute-start.5 = (f32[16,1,32,128]{3,2,1,0:T(8,128)S(1)}, f32[16,1,32,128]{3,2,1,0:T(8,128)S(1)}, u32[]{:S(2)}, u32[]{:S(2)}) collective-permute-start(f32[16,1,32,128]{3,2,1,0:T(8,128)S(1)} %get-tuple-element.28), channel_id=1, source_target_pairs={{0,4},{4,8},{8,12},{12,16},{16,20},{20,24},{24,28},{1,5},{5,9},{9,... | collective-permute-start | bytes 786440 | tf_op jit(solution)/shard_map/ppermute | solution.py:18
  27.7 10.1 %collective-permute-start.4 = (f32[16,1,32,128]{3,2,1,0:T(8,128)S(1)}, f32[16,1,32,128]{3,2,1,0:T(8,128)S(1)}, u32[]{:S(2)}, u32[]{:S(2)}) collective-permute-start(f32[16,1,32,128]{3,2,1,0:T(8,128)S(1)} %get-tuple-element.29), channel_id=1, source_target_pairs={{4,0},{8,4},{12,8},{16,12},{20,16},{24,20},{28,24},{5,1},{9,5},{13... | collective-permute-start | bytes 786440 | tf_op jit(solution)/shard_map/ppermute | solution.py:19
  41.4 23.2 %collective-permute-start.10 = (f32[16,8,1,128]{3,2,1,0:T(1,128)S(1)}, f32[16,8,1,128]{3,2,1,0:T(1,128)S(1)}, u32[]{:S(2)}, u32[]{:S(2)}) collective-permute-start(f32[16,8,1,128]{3,2,1,0:T(1,128)S(1)} %get-tuple-element.22), channel_id=1, source_target_pairs={{1,0},{2,1},{3,2},{5,4},{6,5},{7,6},{9,8},{10,9},{11,10},{13,12},{... | collective-permute-start | bytes 196616 | tf_op jit(solution)/shard_map/ppermute | solution.py:19
  42.7 21.9 %collective-permute-start.11 = (f32[16,8,1,128]{3,2,1,0:T(1,128)S(1)}, f32[16,8,1,128]{3,2,1,0:T(1,128)S(1)}, u32[]{:S(2)}, u32[]{:S(2)}) collective-permute-start(f32[16,8,1,128]{3,2,1,0:T(1,128)S(1)} %get-tuple-element.23), channel_id=1, source_target_pairs={{0,1},{1,2},{2,3},{4,5},{5,6},{6,7},{8,9},{9,10},{10,11},{12,13},{... | collective-permute-start | bytes 196616 | tf_op jit(solution)/shard_map/ppermute | solution.py:18
  47.6 10.0 %collective-permute-start.9 = (f32[16,1,32,128]{3,2,1,0:T(8,128)S(1)}, f32[16,1,32,128]{3,2,1,0:T(8,128)S(1)}, u32[]{:S(2)}, u32[]{:S(2)}) collective-permute-start(f32[16,1,32,128]{3,2,1,0:T(8,128)S(1)} %get-tuple-element.24), channel_id=1, source_target_pairs={{0,4},{4,8},{8,12},{12,16},{16,20},{20,24},{24,28},{1,5},{5,9},{9,... | collective-permute-start | bytes 786440 | tf_op jit(solution)/shard_map/ppermute | solution.py:18
  51.7 12.6 %collective-permute-start.8 = (f32[16,1,32,128]{3,2,1,0:T(8,128)S(1)}, f32[16,1,32,128]{3,2,1,0:T(8,128)S(1)}, u32[]{:S(2)}, u32[]{:S(2)}) collective-permute-start(f32[16,1,32,128]{3,2,1,0:T(8,128)S(1)} %get-tuple-element.25), channel_id=1, source_target_pairs={{4,0},{8,4},{12,8},{16,12},{20,16},{24,20},{28,24},{5,1},{9,5},{13... | collective-permute-start | bytes 786440 | tf_op jit(solution)/shard_map/ppermute | solution.py:19
  67.5 22.2 %collective-permute-start.14 = (f32[16,8,1,128]{3,2,1,0:T(1,128)S(1)}, f32[16,8,1,128]{3,2,1,0:T(1,128)S(1)}, u32[]{:S(2)}, u32[]{:S(2)}) collective-permute-start(f32[16,8,1,128]{3,2,1,0:T(1,128)S(1)} %get-tuple-element.18), channel_id=1, source_target_pairs={{1,0},{2,1},{3,2},{5,4},{6,5},{7,6},{9,8},{10,9},{11,10},{13,12},{... | collective-permute-start | bytes 196616 | tf_op jit(solution)/shard_map/ppermute | solution.py:19
  68.8 20.9 %collective-permute-start.15 = (f32[16,8,1,128]{3,2,1,0:T(1,128)S(1)}, f32[16,8,1,128]{3,2,1,0:T(1,128)S(1)}, u32[]{:S(2)}, u32[]{:S(2)}) collective-permute-start(f32[16,8,1,128]{3,2,1,0:T(1,128)S(1)} %get-tuple-element.19), channel_id=1, source_target_pairs={{0,1},{1,2},{2,3},{4,5},{5,6},{6,7},{8,9},{9,10},{10,11},{12,13},{... | collective-permute-start | bytes 196616 | tf_op jit(solution)/shard_map/ppermute | solution.py:18
  71.9 11.4 %collective-permute-start.13 = (f32[16,1,32,128]{3,2,1,0:T(8,128)S(1)}, f32[16,1,32,128]{3,2,1,0:T(8,128)S(1)}, u32[]{:S(2)}, u32[]{:S(2)}) collective-permute-start(f32[16,1,32,128]{3,2,1,0:T(8,128)S(1)} %get-tuple-element.20), channel_id=1, source_target_pairs={{0,4},{4,8},{8,12},{12,16},{16,20},{20,24},{24,28},{1,5},{5,9},{9,... | collective-permute-start | bytes 786440 | tf_op jit(solution)/shard_map/ppermute | solution.py:18
  76.9 12.5 %collective-permute-start.12 = (f32[16,1,32,128]{3,2,1,0:T(8,128)S(1)}, f32[16,1,32,128]{3,2,1,0:T(8,128)S(1)}, u32[]{:S(2)}, u32[]{:S(2)}) collective-permute-start(f32[16,1,32,128]{3,2,1,0:T(8,128)S(1)} %get-tuple-element.21), channel_id=1, source_target_pairs={{4,0},{8,4},{12,8},{16,12},{20,16},{24,20},{28,24},{5,1},{9,5},{13... | collective-permute-start | bytes 786440 | tf_op jit(solution)/shard_map/ppermute | solution.py:19
  93.5 22.3 %collective-permute-start.18 = (f32[16,8,1,128]{3,2,1,0:T(1,128)S(1)}, f32[16,8,1,128]{3,2,1,0:T(1,128)S(1)}, u32[]{:S(2)}, u32[]{:S(2)}) collective-permute-start(f32[16,8,1,128]{3,2,1,0:T(1,128)S(1)} %get-tuple-element.14), channel_id=1, source_target_pairs={{1,0},{2,1},{3,2},{5,4},{6,5},{7,6},{9,8},{10,9},{11,10},{13,12},{... | collective-permute-start | bytes 196616 | tf_op jit(solution)/shard_map/ppermute | solution.py:19
  94.8 21.1 %collective-permute-start.19 = (f32[16,8,1,128]{3,2,1,0:T(1,128)S(1)}, f32[16,8,1,128]{3,2,1,0:T(1,128)S(1)}, u32[]{:S(2)}, u32[]{:S(2)}) collective-permute-start(f32[16,8,1,128]{3,2,1,0:T(1,128)S(1)} %get-tuple-element.15), channel_id=1, source_target_pairs={{0,1},{1,2},{2,3},{4,5},{5,6},{6,7},{8,9},{9,10},{10,11},{12,13},{... | collective-permute-start | bytes 196616 | tf_op jit(solution)/shard_map/ppermute | solution.py:18
  97.8 11.4 %collective-permute-start.17 = (f32[16,1,32,128]{3,2,1,0:T(8,128)S(1)}, f32[16,1,32,128]{3,2,1,0:T(8,128)S(1)}, u32[]{:S(2)}, u32[]{:S(2)}) collective-permute-start(f32[16,1,32,128]{3,2,1,0:T(8,128)S(1)} %get-tuple-element.16), channel_id=1, source_target_pairs={{0,4},{4,8},{8,12},{12,16},{16,20},{20,24},{24,28},{1,5},{5,9},{9,... | collective-permute-start | bytes 786440 | tf_op jit(solution)/shard_map/ppermute | solution.py:18
  102.9 12.5 %collective-permute-start.16 = (f32[16,1,32,128]{3,2,1,0:T(8,128)S(1)}, f32[16,1,32,128]{3,2,1,0:T(8,128)S(1)}, u32[]{:S(2)}, u32[]{:S(2)}) collective-permute-start(f32[16,1,32,128]{3,2,1,0:T(8,128)S(1)} %get-tuple-element.17), channel_id=1, source_target_pairs={{4,0},{8,4},{12,8},{16,12},{20,16},{24,20},{28,24},{5,1},{9,5},{13... | collective-permute-start | bytes 786440 | tf_op jit(solution)/shard_map/ppermute | solution.py:19
  123.0 22.2 %collective-permute-start.22 = (f32[16,8,1,128]{3,2,1,0:T(1,128)S(1)}, f32[16,8,1,128]{3,2,1,0:T(1,128)S(1)}, u32[]{:S(2)}, u32[]{:S(2)}) collective-permute-start(f32[16,8,1,128]{3,2,1,0:T(1,128)S(1)} %get-tuple-element.10), channel_id=1, source_target_pairs={{1,0},{2,1},{3,2},{5,4},{6,5},{7,6},{9,8},{10,9},{11,10},{13,12},{... | collective-permute-start | bytes 196616 | tf_op jit(solution)/shard_map/ppermute | solution.py:19
  124.2 21.0 %collective-permute-start.23 = (f32[16,8,1,128]{3,2,1,0:T(1,128)S(1)}, f32[16,8,1,128]{3,2,1,0:T(1,128)S(1)}, u32[]{:S(2)}, u32[]{:S(2)}) collective-permute-start(f32[16,8,1,128]{3,2,1,0:T(1,128)S(1)} %get-tuple-element.11), channel_id=1, source_target_pairs={{0,1},{1,2},{2,3},{4,5},{5,6},{6,7},{8,9},{9,10},{10,11},{12,13},{... | collective-permute-start | bytes 196616 | tf_op jit(solution)/shard_map/ppermute | solution.py:18
  127.3 11.4 %collective-permute-start.21 = (f32[16,1,32,128]{3,2,1,0:T(8,128)S(1)}, f32[16,1,32,128]{3,2,1,0:T(8,128)S(1)}, u32[]{:S(2)}, u32[]{:S(2)}) collective-permute-start(f32[16,1,32,128]{3,2,1,0:T(8,128)S(1)} %get-tuple-element.12), channel_id=1, source_target_pairs={{0,4},{4,8},{8,12},{12,16},{16,20},{20,24},{24,28},{1,5},{5,9},{9,... | collective-permute-start | bytes 786440 | tf_op jit(solution)/shard_map/ppermute | solution.py:18
  132.3 12.5 %collective-permute-start.20 = (f32[16,1,32,128]{3,2,1,0:T(8,128)S(1)}, f32[16,1,32,128]{3,2,1,0:T(8,128)S(1)}, u32[]{:S(2)}, u32[]{:S(2)}) collective-permute-start(f32[16,1,32,128]{3,2,1,0:T(8,128)S(1)} %get-tuple-element.13), channel_id=1, source_target_pairs={{4,0},{8,4},{12,8},{16,12},{20,16},{24,20},{28,24},{5,1},{9,5},{13... | collective-permute-start | bytes 786440 | tf_op jit(solution)/shard_map/ppermute | solution.py:19
  (9 other events, 31.4 us)

commit v2 on v1

--- a/solution.py
+++ b/solution.py
@@ -4,6 +4,7 @@
 from jax.sharding import PartitionSpec as P
 
 FILTER_STEPS = 2
+CHUNKS = 2
 
 
 FILTER_CENTRE = 22.0
@@ -87,7 +88,6 @@
 
 def on_device(start_panel, ocean_mask, conduct_x, conduct_y, conduct_z, diag_shift):
     ocean_cells = ocean_mask.astype(jnp.float32)
-    fields = jnp.stack([ocean_cells, conduct_x, conduct_y, conduct_z, diag_shift])
     vectors = start_panel.shape[0]
     cell_total = (
         start_panel.shape[1]
@@ -96,13 +96,36 @@
         * lax.axis_size("gx")
         * lax.axis_size("gy")
     )
-    field = start_panel * ocean_cells[None]
-    fields_one = padded_2(fields, (("gx", 1), ("gy", 2)), 1)
-    for repeat in range(FILTER_STEPS):
-        middle = (operate(field, fields_one) - FILTER_CENTRE * field) / FILTER_HALF
-        field = (
-            2.0 * (operate(middle, fields_one) - FILTER_CENTRE * middle) / FILTER_HALF - field
-        ) / FILTER_NORM
+    start_field = start_panel * ocean_cells[None]
+    share = vectors // CHUNKS
+    fields_one = None
+    fields_done = []
+    images_done = []
+    for chunk in range(CHUNKS):
+        field = start_field[chunk * share : (chunk + 1) * share]
+        if fields_one is None:
+            together = padded_2(
+                jnp.concatenate(
+                    [field, jnp.stack([ocean_cells, conduct_x, conduct_y, conduct_z, diag_shift])]
+                ),
+                (("gx", 1), ("gy", 2)),
+                1,
+            )
+            fields_one = together[share:]
+            applied = stencil(together[:share], fields_one)
+        else:
+            applied = operate(field, fields_one)
+        for repeat in range(FILTER_STEPS):
+            if repeat:
+                applied = operate(field, fields_one)
+            middle = (applied - FILTER_CENTRE * field) / FILTER_HALF
+            field = (
+                2.0 * (operate(middle, fields_one) - FILTER_CENTRE * middle) / FILTER_HALF - field
+            ) / FILTER_NORM
+        fields_done.append(field)
+        images_done.append(operate(field, fields_one))
+    field = jnp.concatenate(fields_done)
+    raw_images = jnp.concatenate(images_done).reshape(vectors, -1)
     flattened = field.reshape(vectors, -1)
     raw_images = operate(field, fields_one).reshape(vectors, -1)
     sums = reduce_all(

time: 190 us -> 202 us (1.063)
  starting transfers between devices: 75 us -> 119 us
  waiting for transfers between devices: 60 us -> 23.9 us
  local copies, waits for them, and re-layouts: 9.45 us -> 17.1 us
  other arithmetic: 26.6 us -> 23.4 us
    ppermute x12 -> x18, starting transfers between devices: 48.7 us -> 82.1 us  [halo_pair(): lax.ppermute(lax.slice_in_dim(block, block.shape[dim] - 1, None, axis=dim...]
    ppermute x12 -> x18, waiting for transfers between devices: 30 us -> 10.6 us  [halo_pair(): high = lax.ppermute(lax.slice_in_dim(block, 0, 1, axis=dim), axis, backward)]
    ppermute x12 -> x18, waiting for transfers between devices: 20.1 us -> 6.95 us  [halo_pair(): lax.ppermute(lax.slice_in_dim(block, block.shape[dim] - 1, None, axis=dim...]
    concatenate x0 -> x2, local copies, waits for them, and re-layouts: none -> 8.71 us  [the longest x1 6.75 us: on_device(): jnp.concatenate([field, jnp.stack([ocean_cells, conduct_x, conduct_y, con...]
    ppermute x12 -> x18, starting transfers between devices: 15.7 us -> 23.4 us  [halo_pair(): high = lax.ppermute(lax.slice_in_dim(block, 0, 1, axis=dim), axis, backward)]
    unnamed x13 -> x11, local copies, waits for them, and re-layouts: 7.67 us -> 3.51 us
    ppermute x5, waiting for transfers between devices: 9.94 us -> 6.33 us  [reduce_all(): value = value + lax.ppermute(value, axis, pairs)]
    ppermute x5, starting transfers between devices: 10.7 us -> 13.6 us  [reduce_all(): value = value + lax.ppermute(value, axis, pairs)]
  transfers between devices with their start and end apart: 29 -> 41, of which waited for: 15 -> 11; matrix products, arithmetic and copies ran while one was open for 4% -> 8% of each run, Pallas kernels for 0% -> 0%
where the time goes in v2:
time: 202 us; the launch traced here: 200 us
  starting transfers between devices  119 us (59%)
  waiting for transfers between devices  23.9 us (12%)
  other arithmetic  23.4 us (12%)
  local copies, waits for them, and re-layouts  17.1 us (8%)
  matrix products  15.4 us (8%)
    ppermute x18, starting transfers between devices, halo_pair(): lax.ppermute(lax.slice_in_dim(block, block.shape[dim] - 1, None, axis=dim...  82.1 us
    ppermute x18, starting transfers between devices, halo_pair(): high = lax.ppermute(lax.slice_in_dim(block, 0, 1, axis=dim), axis, backward)  23.4 us
    ppermute x5, starting transfers between devices, reduce_all(): value = value + lax.ppermute(value, axis, pairs)  13.6 us
    ppermute x18, waiting for transfers between devices, halo_pair(): high = lax.ppermute(lax.slice_in_dim(block, 0, 1, axis=dim), axis, backward)  10.6 us
    dot_general x3, matrix products, combine(): jnp.einsum('kl,lc->kc', matrix, rows, precision=lax.Precision.HIGHEST)  9.13 us
    ppermute x18, waiting for transfers between devices, halo_pair(): lax.ppermute(lax.slice_in_dim(block, block.shape[dim] - 1, None, axis=dim...  6.95 us
    concatenate x1, local copies, waits for them, and re-layouts, on_device(): jnp.concatenate([field, jnp.stack([ocean_cells, conduct_x, conduct_y, con...  6.75 us
    ppermute x5, waiting for transfers between devices, reduce_all(): value = value + lax.ppermute(value, axis, pairs)  6.33 us
  transfers between devices with their start and end apart: 41, of which 11 were waited for; matrix products, arithmetic and copies ran while one was open for 8% of the time, Pallas kernels for 0%

profile of v2, /device:TPU:0, one launch (start us, length us, event | category | flops | bytes accessed | tf_op | source)
XLA Modules:
  0.0 200.5 jit_solution(7795700380861102761)
XLA Ops:
  7.7 6.7 %concatenate.152 = f32[13,8,32,128]{3,0,2,1:T(8,128)} concatenate(f32[8,8,32,128]{3,0,2,1:T(8,128)} %get-tuple-element.36, f32[1,8,32,128]{3,0,2,1:T(1,128)S(1)} %bitcast.71, f32[1,8,32,128]{3,0,2,1:T(1,128)S(1)} %bitcast.75, f32[1,8,32,128]{3,0,2,1:T(1,128)S(1)} %bitcast.76, f32[1,8,32,128]{3,0,2,1:T(1,128)} %bitcast.77, f32[1,8,32,128]{3,0,2,1:T(1,128)} %bitcast.78), dimensions={0} | concatenate | bytes 3407872 | tf_op jit(solution)/shard_map/concatenate | solution.py:108
  15.5 3.0 %collective-permute-start = (f32[13,8,1,128]{3,0,2,1:T(8,128)S(1)}, f32[13,8,1,128]{3,0,2,1:T(8,128)S(1)}, u32[]{:S(2)}, u32[]{:S(2)}) collective-permute-start(f32[13,8,1,128]{3,0,2,1:T(8,128)S(1)} %get-tuple-element.39), channel_id=1, source_target_pairs={{0,1},{1,2},{2,3},{4,5},{5,6},{6,7},{8,9},{9,10},{10,11},{12,13},{... | collective-permute-start | bytes 159752 | tf_op jit(solution)/shard_map/ppermute | solution.py:19
  20.9 4.9 %collective-permute-start.1 = (f32[13,1,32,128]{3,0,2,1:T(8,128)S(1)}, f32[13,1,32,128]{3,0,2,1:T(8,128)S(1)}, u32[]{:S(2)}, u32[]{:S(2)}) collective-permute-start(f32[13,1,32,128]{3,0,2,1:T(8,128)S(1)} %get-tuple-element.37), channel_id=1, source_target_pairs={{0,4},{4,8},{8,12},{12,16},{16,20},{20,24},{24,28},{1,5},{5,9},{9,... | collective-permute-start | bytes 638984 | tf_op jit(solution)/shard_map/ppermute | solution.py:19
  27.1 3.4 %collective-permute-start.19 = (f32[8,8,1,128]{3,0,2,1:T(8,128)}, f32[8,8,1,128]{3,0,2,1:T(8,128)S(1)}, u32[]{:S(2)}, u32[]{:S(2)}) collective-permute-start(f32[8,8,1,128]{3,0,2,1:T(8,128)} %get-tuple-element.32), channel_id=1, source_target_pairs={{0,1},{1,2},{2,3},{4,5},{5,6},{6,7},{8,9},{9,10},{10,11},{12,13},{... | collective-permute-start | bytes 98312 | tf_op jit(solution)/shard_map/ppermute | solution.py:19
  30.5 4.3 %collective-permute-start.17 = (f32[8,1,32,128]{3,0,2,1:T(8,128)S(1)}, f32[8,1,32,128]{3,0,2,1:T(8,128)S(1)}, u32[]{:S(2)}, u32[]{:S(2)}) collective-permute-start(f32[8,1,32,128]{3,0,2,1:T(8,128)S(1)} %get-tuple-element.33), channel_id=1, source_target_pairs={{0,4},{4,8},{8,12},{12,16},{16,20},{20,24},{24,28},{1,5},{5,9},{9,... | collective-permute-start | bytes 393224 | tf_op jit(solution)/shard_map/ppermute | solution.py:19
  40.2 5.0 %collective-permute-done.16 = f32[8,1,32,128]{3,0,2,1:T(8,128)S(1)} collective-permute-done((f32[8,1,32,128]{3,0,2,1:T(8,128)S(1)}, f32[8,1,32,128]{3,0,2,1:T(8,128)S(1)}, u32[]{:S(2)}, u32[]{:S(2)}) %collective-permute-start.16) | collective-permute-done | bytes 131104 | tf_op jit(solution)/shard_map/ppermute | solution.py:20
  50.0 5.1 %collective-permute-start.21 = (f32[8,1,32,128]{3,0,2,1:T(8,128)S(1)}, f32[8,1,32,128]{3,0,2,1:T(8,128)S(1)}, u32[]{:S(2)}, u32[]{:S(2)}) collective-permute-start(f32[8,1,32,128]{3,0,2,1:T(8,128)S(1)} %get-tuple-element.51), channel_id=1, source_target_pairs={{0,4},{4,8},{8,12},{12,16},{16,20},{20,24},{24,28},{1,5},{5,9},{9,... | collective-permute-start | bytes 393224 | tf_op jit(solution)/shard_map/ppermute | solution.py:19
  56.4 4.6 %collective-permute-start.5 = (f32[8,1,32,128]{3,0,2,1:T(8,128)S(1)}, f32[8,1,32,128]{3,0,2,1:T(8,128)S(1)}, u32[]{:S(2)}, u32[]{:S(2)}) collective-permute-start(f32[8,1,32,128]{3,0,2,1:T(8,128)S(1)} %get-tuple-element.63), channel_id=1, source_target_pairs={{0,4},{4,8},{8,12},{12,16},{16,20},{20,24},{24,28},{1,5},{5,9},{9,... | collective-permute-start | bytes 393224 | tf_op jit(solution)/shard_map/ppermute | solution.py:19
  65.9 6.3 %collective-permute-start.7 = (f32[8,8,1,128]{3,0,2,1:T(8,128)S(1)}, f32[8,8,1,128]{3,0,2,1:T(8,128)S(1)}, u32[]{:S(2)}, u32[]{:S(2)}) collective-permute-start(f32[8,8,1,128]{3,0,2,1:T(8,128)S(1)} %get-tuple-element.62), channel_id=1, source_target_pairs={{0,1},{1,2},{2,3},{4,5},{5,6},{6,7},{8,9},{9,10},{10,11},{12,13},{... | collective-permute-start | bytes 98312 | tf_op jit(solution)/shard_map/ppermute | solution.py:19
  76.9 4.6 %collective-permute-start.25 = (f32[8,1,32,128]{3,0,2,1:T(8,128)S(1)}, f32[8,1,32,128]{3,0,2,1:T(8,128)S(1)}, u32[]{:S(2)}, u32[]{:S(2)}) collective-permute-start(f32[8,1,32,128]{3,0,2,1:T(8,128)S(1)} %get-tuple-element.47), channel_id=1, source_target_pairs={{0,4},{4,8},{8,12},{12,16},{16,20},{20,24},{24,28},{1,5},{5,9},{9,... | collective-permute-start | bytes 393224 | tf_op jit(solution)/shard_map/ppermute | solution.py:19
  82.8 4.6 %collective-permute-start.9 = (f32[8,1,32,128]{3,0,2,1:T(8,128)S(1)}, f32[8,1,32,128]{3,0,2,1:T(8,128)S(1)}, u32[]{:S(2)}, u32[]{:S(2)}) collective-permute-start(f32[8,1,32,128]{3,0,2,1:T(8,128)S(1)} %get-tuple-element.59), channel_id=1, source_target_pairs={{0,4},{4,8},{8,12},{12,16},{16,20},{20,24},{24,28},{1,5},{5,9},{9,... | collective-permute-start | bytes 393224 | tf_op jit(solution)/shard_map/ppermute | solution.py:19
  88.6 3.8 %collective-permute-start.27 = (f32[8,8,1,128]{3,0,2,1:T(8,128)S(1)}, f32[8,8,1,128]{3,0,2,1:T(8,128)S(1)}, u32[]{:S(2)}, u32[]{:S(2)}) collective-permute-start(f32[8,8,1,128]{3,0,2,1:T(8,128)S(1)} %get-tuple-element.46), channel_id=1, source_target_pairs={{0,1},{1,2},{2,3},{4,5},{5,6},{6,7},{8,9},{9,10},{10,11},{12,13},{... | collective-permute-start | bytes 98312 | tf_op jit(solution)/shard_map/ppermute | solution.py:19
  93.8 5.5 %collective-permute-start.11 = (f32[8,8,1,128]{3,0,2,1:T(8,128)S(1)}, f32[8,8,1,128]{3,0,2,1:T(8,128)S(1)}, u32[]{:S(2)}, u32[]{:S(2)}) collective-permute-start(f32[8,8,1,128]{3,0,2,1:T(8,128)S(1)} %get-tuple-element.58), channel_id=1, source_target_pairs={{0,1},{1,2},{2,3},{4,5},{5,6},{6,7},{8,9},{9,10},{10,11},{12,13},{... | collective-permute-start | bytes 98312 | tf_op jit(solution)/shard_map/ppermute | solution.py:19
  103.9 5.4 %collective-permute-start.29 = (f32[8,1,32,128]{3,0,2,1:T(8,128)S(1)}, f32[8,1,32,128]{3,0,2,1:T(8,128)S(1)}, u32[]{:S(2)}, u32[]{:S(2)}) collective-permute-start(f32[8,1,32,128]{3,0,2,1:T(8,128)S(1)} %get-tuple-element.43), channel_id=1, source_target_pairs={{0,4},{4,8},{8,12},{12,16},{16,20},{20,24},{24,28},{1,5},{5,9},{9,... | collective-permute-start | bytes 393224 | tf_op jit(solution)/shard_map/ppermute | solution.py:19
  110.6 5.4 %collective-permute-start.13 = (f32[8,1,32,128]{3,0,2,1:T(8,128)S(1)}, f32[8,1,32,128]{3,0,2,1:T(8,128)S(1)}, u32[]{:S(2)}, u32[]{:S(2)}) collective-permute-start(f32[8,1,32,128]{3,0,2,1:T(8,128)S(1)} %get-tuple-element.55), channel_id=1, source_target_pairs={{0,4},{4,8},{8,12},{12,16},{16,20},{20,24},{24,28},{1,5},{5,9},{9,... | collective-permute-start | bytes 393224 | tf_op jit(solution)/shard_map/ppermute | solution.py:19
  117.4 3.9 %collective-permute-start.31 = (f32[8,8,1,128]{3,0,2,1:T(8,128)S(1)}, f32[8,8,1,128]{3,0,2,1:T(8,128)S(1)}, u32[]{:S(2)}, u32[]{:S(2)}) collective-permute-start(f32[8,8,1,128]{3,0,2,1:T(8,128)S(1)} %get-tuple-element.42), channel_id=1, source_target_pairs={{0,1},{1,2},{2,3},{4,5},{5,6},{6,7},{8,9},{9,10},{10,11},{12,13},{... | collective-permute-start | bytes 98312 | tf_op jit(solution)/shard_map/ppermute | solution.py:19
  122.6 5.6 %collective-permute-start.15 = (f32[8,8,1,128]{3,0,2,1:T(8,128)S(1)}, f32[8,8,1,128]{3,0,2,1:T(8,128)S(1)}, u32[]{:S(2)}, u32[]{:S(2)}) collective-permute-start(f32[8,8,1,128]{3,0,2,1:T(8,128)S(1)} %get-tuple-element.54), channel_id=1, source_target_pairs={{0,1},{1,2},{2,3},{4,5},{5,6},{6,7},{8,9},{9,10},{10,11},{12,13},{... | collective-permute-start | bytes 98312 | tf_op jit(solution)/shard_map/ppermute | solution.py:19
  135.0 4.4 %collective-permute-start.35 = (f32[16,8,1,128]{3,0,2,1:T(8,128)S(1)}, f32[16,8,1,128]{3,0,2,1:T(8,128)S(1)}, u32[]{:S(2)}, u32[]{:S(2)}) collective-permute-start(f32[16,8,1,128]{3,0,2,1:T(8,128)S(1)} %get-tuple-element.28), channel_id=1, source_target_pairs={{0,1},{1,2},{2,3},{4,5},{5,6},{6,7},{8,9},{9,10},{10,11},{12,13},{... | collective-permute-start | bytes 196616 | tf_op jit(solution)/shard_map/ppermute | solution.py:19
  139.4 5.3 %collective-permute-start.33 = (f32[16,1,32,128]{3,0,2,1:T(8,128)S(1)}, f32[16,1,32,128]{3,0,2,1:T(8,128)S(1)}, u32[]{:S(2)}, u32[]{:S(2)}) collective-permute-start(f32[16,1,32,128]{3,0,2,1:T(8,128)S(1)} %get-tuple-element.29), channel_id=1, source_target_pairs={{0,4},{4,8},{8,12},{12,16},{16,20},{20,24},{24,28},{1,5},{5,9},{9,... | collective-permute-start | bytes 786440 | tf_op jit(solution)/shard_map/ppermute | solution.py:19
  146.7 3.2 %collective-permute-done.33 = f32[16,1,32,128]{3,0,2,1:T(8,128)S(1)} collective-permute-done((f32[16,1,32,128]{3,0,2,1:T(8,128)S(1)}, f32[16,1,32,128]{3,0,2,1:T(8,128)S(1)}, u32[]{:S(2)}, u32[]{:S(2)}) %collective-permute-start.33) | collective-permute-done | bytes 262176 | tf_op jit(solution)/shard_map/ppermute | solution.py:19
  149.8 5.6 %collective-permute-done.32 = f32[16,1,32,128]{3,0,2,1:T(8,128)S(1)} collective-permute-done((f32[16,1,32,128]{3,0,2,1:T(8,128)S(1)}, f32[16,1,32,128]{3,0,2,1:T(8,128)S(1)}, u32[]{:S(2)}, u32[]{:S(2)}) %collective-permute-start.32) | collective-permute-done | bytes 262176 | tf_op jit(solution)/shard_map/ppermute | solution.py:20
  171.1 4.7 %collective-permute-start.39 = (f32[2,16,16]{1,2,0:T(8,128)S(1)}, f32[2,16,16]{1,2,0:T(8,128)S(1)}, u32[]{:S(2)}, u32[]{:S(2)}) collective-permute-start(f32[2,16,16]{1,2,0:T(8,128)S(1)} %add.208), channel_id=1, source_target_pairs={{0,8},{4,12},{8,0},{12,4},{16,24},{20,28},{24,16},{28,20},{1,9},{5... | collective-permute-start | bytes 6152 | tf_op jit(solution)/shard_map/ppermute | solution.py:69
  177.6 3.0 %collective-permute-start.40 = (f32[2,16,16]{1,2,0:T(8,128)S(1)}, f32[2,16,16]{1,2,0:T(8,128)S(1)}, u32[]{:S(2)}, u32[]{:S(2)}) collective-permute-start(f32[2,16,16]{1,2,0:T(8,128)S(1)} %add.209), channel_id=1, source_target_pairs={{0,16},{4,20},{8,24},{12,28},{16,0},{20,4},{24,8},{28,12},{1,17},{... | collective-permute-start | bytes 6152 | tf_op jit(solution)/shard_map/ppermute | solution.py:69
  187.7 4.4 %fusion.12 = f32[16,32768]{1,0:T(8,128)S(1)} fusion(f32[16,16]{1,0:T(8,128)S(1)} %fusion.126, f32[2,8,256,128]{3,2,1,0:T(8,128)} %bitcast.68), kind=kOutput, calls=%fused_computation.37 | convolution fusion | flops 100663296 | bytes 4195328 | tf_op jit(solution)/shard_map/kl,lc->kc/dot_general | solution.py:79
  (145 shorter events, 86.3 us)
Async XLA Ops:
  5.1 40.5 %collective-permute-start.18 = (f32[8,8,1,128]{3,0,2,1:T(8,128)}, f32[8,8,1,128]{3,0,2,1:T(8,128)}, u32[]{:S(2)}, u32[]{:S(2)}) collective-permute-start(f32[8,8,1,128]{3,0,2,1:T(8,128)} %get-tuple-element.31), channel_id=1, source_target_pairs={{1,0},{2,1},{3,2},{5,4},{6,5},{7,6},{9,8},{10,9},{11,10},{13,12},{... | collective-permute-start | bytes 98312 | tf_op jit(solution)/shard_map/ppermute | solution.py:20
  15.5 11.6 %collective-permute-start = (f32[13,8,1,128]{3,0,2,1:T(8,128)S(1)}, f32[13,8,1,128]{3,0,2,1:T(8,128)S(1)}, u32[]{:S(2)}, u32[]{:S(2)}) collective-permute-start(f32[13,8,1,128]{3,0,2,1:T(8,128)S(1)} %get-tuple-element.39), channel_id=1, source_target_pairs={{0,1},{1,2},{2,3},{4,5},{5,6},{6,7},{8,9},{9,10},{10,11},{12,13},{... | collective-permute-start | bytes 159752 | tf_op jit(solution)/shard_map/ppermute | solution.py:19
  18.5 12.0 %collective-permute-start.3 = (f32[13,8,1,128]{3,0,2,1:T(8,128)S(1)}, f32[13,8,1,128]{3,0,2,1:T(8,128)S(1)}, u32[]{:S(2)}, u32[]{:S(2)}) collective-permute-start(f32[13,8,1,128]{3,0,2,1:T(8,128)S(1)} %get-tuple-element.40), channel_id=1, source_target_pairs={{1,0},{2,1},{3,2},{5,4},{6,5},{7,6},{9,8},{10,9},{11,10},{13,12},{... | collective-permute-start | bytes 159752 | tf_op jit(solution)/shard_map/ppermute | solution.py:20
  20.9 16.3 %collective-permute-start.1 = (f32[13,1,32,128]{3,0,2,1:T(8,128)S(1)}, f32[13,1,32,128]{3,0,2,1:T(8,128)S(1)}, u32[]{:S(2)}, u32[]{:S(2)}) collective-permute-start(f32[13,1,32,128]{3,0,2,1:T(8,128)S(1)} %get-tuple-element.37), channel_id=1, source_target_pairs={{0,4},{4,8},{8,12},{12,16},{16,20},{20,24},{24,28},{1,5},{5,9},{9,... | collective-permute-start | bytes 638984 | tf_op jit(solution)/shard_map/ppermute | solution.py:19
  25.8 12.7 %collective-permute-start.2 = (f32[13,1,32,128]{3,0,2,1:T(8,128)S(1)}, f32[13,1,32,128]{3,0,2,1:T(8,128)S(1)}, u32[]{:S(2)}, u32[]{:S(2)}) collective-permute-start(f32[13,1,32,128]{3,0,2,1:T(8,128)S(1)} %get-tuple-element.38), channel_id=1, source_target_pairs={{4,0},{8,4},{12,8},{16,12},{20,16},{24,20},{28,24},{5,1},{9,5},{13... | collective-permute-start | bytes 638984 | tf_op jit(solution)/shard_map/ppermute | solution.py:20
  27.1 18.4 %collective-permute-start.19 = (f32[8,8,1,128]{3,0,2,1:T(8,128)}, f32[8,8,1,128]{3,0,2,1:T(8,128)S(1)}, u32[]{:S(2)}, u32[]{:S(2)}) collective-permute-start(f32[8,8,1,128]{3,0,2,1:T(8,128)} %get-tuple-element.32), channel_id=1, source_target_pairs={{0,1},{1,2},{2,3},{4,5},{5,6},{6,7},{8,9},{9,10},{10,11},{12,13},{... | collective-permute-start | bytes 98312 | tf_op jit(solution)/shard_map/ppermute | solution.py:19
  48.7 23.7 %collective-permute-start.22 = (f32[8,8,1,128]{3,0,2,1:T(8,128)S(1)}, f32[8,8,1,128]{3,0,2,1:T(8,128)S(1)}, u32[]{:S(2)}, u32[]{:S(2)}) collective-permute-start(f32[8,8,1,128]{3,0,2,1:T(8,128)S(1)} %get-tuple-element.49), channel_id=1, source_target_pairs={{1,0},{2,1},{3,2},{5,4},{6,5},{7,6},{9,8},{10,9},{11,10},{13,12},{... | collective-permute-start | bytes 98312 | tf_op jit(solution)/shard_map/ppermute | solution.py:20
  50.0 12.3 %collective-permute-start.21 = (f32[8,1,32,128]{3,0,2,1:T(8,128)S(1)}, f32[8,1,32,128]{3,0,2,1:T(8,128)S(1)}, u32[]{:S(2)}, u32[]{:S(2)}) collective-permute-start(f32[8,1,32,128]{3,0,2,1:T(8,128)S(1)} %get-tuple-element.51), channel_id=1, source_target_pairs={{0,4},{4,8},{8,12},{12,16},{16,20},{20,24},{24,28},{1,5},{5,9},{9,... | collective-permute-start | bytes 393224 | tf_op jit(solution)/shard_map/ppermute | solution.py:19
  61.0 11.1 %collective-permute-start.4 = (f32[8,1,32,128]{3,0,2,1:T(8,128)S(1)}, f32[8,1,32,128]{3,0,2,1:T(8,128)S(1)}, u32[]{:S(2)}, u32[]{:S(2)}) collective-permute-start(f32[8,1,32,128]{3,0,2,1:T(8,128)S(1)} %get-tuple-element.64), channel_id=1, source_target_pairs={{4,0},{8,4},{12,8},{16,12},{20,16},{24,20},{28,24},{5,1},{9,5},{13... | collective-permute-start | bytes 393224 | tf_op jit(solution)/shard_map/ppermute | solution.py:20
  75.6 24.0 %collective-permute-start.26 = (f32[8,8,1,128]{3,0,2,1:T(8,128)S(1)}, f32[8,8,1,128]{3,0,2,1:T(8,128)S(1)}, u32[]{:S(2)}, u32[]{:S(2)}) collective-permute-start(f32[8,8,1,128]{3,0,2,1:T(8,128)S(1)} %get-tuple-element.45), channel_id=1, source_target_pairs={{1,0},{2,1},{3,2},{5,4},{6,5},{7,6},{9,8},{10,9},{11,10},{13,12},{... | collective-permute-start | bytes 98312 | tf_op jit(solution)/shard_map/ppermute | solution.py:20
  76.9 11.7 %collective-permute-start.25 = (f32[8,1,32,128]{3,0,2,1:T(8,128)S(1)}, f32[8,1,32,128]{3,0,2,1:T(8,128)S(1)}, u32[]{:S(2)}, u32[]{:S(2)}) collective-permute-start(f32[8,1,32,128]{3,0,2,1:T(8,128)S(1)} %get-tuple-element.47), channel_id=1, source_target_pairs={{0,4},{4,8},{8,12},{12,16},{16,20},{20,24},{24,28},{1,5},{5,9},{9,... | collective-permute-start | bytes 393224 | tf_op jit(solution)/shard_map/ppermute | solution.py:19
  81.5 11.0 %collective-permute-start.24 = (f32[8,1,32,128]{3,0,2,1:T(8,128)S(1)}, f32[8,1,32,128]{3,0,2,1:T(8,128)S(1)}, u32[]{:S(2)}, u32[]{:S(2)}) collective-permute-start(f32[8,1,32,128]{3,0,2,1:T(8,128)S(1)} %get-tuple-element.48), channel_id=1, source_target_pairs={{4,0},{8,4},{12,8},{16,12},{20,16},{24,20},{28,24},{5,1},{9,5},{13... | collective-permute-start | bytes 393224 | tf_op jit(solution)/shard_map/ppermute | solution.py:20
  82.8 11.0 %collective-permute-start.9 = (f32[8,1,32,128]{3,0,2,1:T(8,128)S(1)}, f32[8,1,32,128]{3,0,2,1:T(8,128)S(1)}, u32[]{:S(2)}, u32[]{:S(2)}) collective-permute-start(f32[8,1,32,128]{3,0,2,1:T(8,128)S(1)} %get-tuple-element.59), channel_id=1, source_target_pairs={{0,4},{4,8},{8,12},{12,16},{16,20},{20,24},{24,28},{1,5},{5,9},{9,... | collective-permute-start | bytes 393224 | tf_op jit(solution)/shard_map/ppermute | solution.py:19
  87.3 11.9 %collective-permute-start.8 = (f32[8,1,32,128]{3,0,2,1:T(8,128)S(1)}, f32[8,1,32,128]{3,0,2,1:T(8,128)S(1)}, u32[]{:S(2)}, u32[]{:S(2)}) collective-permute-start(f32[8,1,32,128]{3,0,2,1:T(8,128)S(1)} %get-tuple-element.60), channel_id=1, source_target_pairs={{4,0},{8,4},{12,8},{16,12},{20,16},{24,20},{28,24},{5,1},{9,5},{13... | collective-permute-start | bytes 393224 | tf_op jit(solution)/shard_map/ppermute | solution.py:20
  88.6 10.9 %collective-permute-start.27 = (f32[8,8,1,128]{3,0,2,1:T(8,128)S(1)}, f32[8,8,1,128]{3,0,2,1:T(8,128)S(1)}, u32[]{:S(2)}, u32[]{:S(2)}) collective-permute-start(f32[8,8,1,128]{3,0,2,1:T(8,128)S(1)} %get-tuple-element.46), channel_id=1, source_target_pairs={{0,1},{1,2},{2,3},{4,5},{5,6},{6,7},{8,9},{9,10},{10,11},{12,13},{... | collective-permute-start | bytes 98312 | tf_op jit(solution)/shard_map/ppermute | solution.py:19
  102.6 25.9 %collective-permute-start.30 = (f32[8,8,1,128]{3,0,2,1:T(8,128)S(1)}, f32[8,8,1,128]{3,0,2,1:T(8,128)S(1)}, u32[]{:S(2)}, u32[]{:S(2)}) collective-permute-start(f32[8,8,1,128]{3,0,2,1:T(8,128)S(1)} %get-tuple-element.41), channel_id=1, source_target_pairs={{1,0},{2,1},{3,2},{5,4},{6,5},{7,6},{9,8},{10,9},{11,10},{13,12},{... | collective-permute-start | bytes 98312 | tf_op jit(solution)/shard_map/ppermute | solution.py:20
  103.9 13.5 %collective-permute-start.29 = (f32[8,1,32,128]{3,0,2,1:T(8,128)S(1)}, f32[8,1,32,128]{3,0,2,1:T(8,128)S(1)}, u32[]{:S(2)}, u32[]{:S(2)}) collective-permute-start(f32[8,1,32,128]{3,0,2,1:T(8,128)S(1)} %get-tuple-element.43), channel_id=1, source_target_pairs={{0,4},{4,8},{8,12},{12,16},{16,20},{20,24},{24,28},{1,5},{5,9},{9,... | collective-permute-start | bytes 393224 | tf_op jit(solution)/shard_map/ppermute | solution.py:19
  109.3 12.0 %collective-permute-start.28 = (f32[8,1,32,128]{3,0,2,1:T(8,128)S(1)}, f32[8,1,32,128]{3,0,2,1:T(8,128)S(1)}, u32[]{:S(2)}, u32[]{:S(2)}) collective-permute-start(f32[8,1,32,128]{3,0,2,1:T(8,128)S(1)} %get-tuple-element.44), channel_id=1, source_target_pairs={{4,0},{8,4},{12,8},{16,12},{20,16},{24,20},{28,24},{5,1},{9,5},{13... | collective-permute-start | bytes 393224 | tf_op jit(solution)/shard_map/ppermute | solution.py:20
  110.6 12.0 %collective-permute-start.13 = (f32[8,1,32,128]{3,0,2,1:T(8,128)S(1)}, f32[8,1,32,128]{3,0,2,1:T(8,128)S(1)}, u32[]{:S(2)}, u32[]{:S(2)}) collective-permute-start(f32[8,1,32,128]{3,0,2,1:T(8,128)S(1)} %get-tuple-element.55), channel_id=1, source_target_pairs={{0,4},{4,8},{8,12},{12,16},{16,20},{20,24},{24,28},{1,5},{5,9},{9,... | collective-permute-start | bytes 393224 | tf_op jit(solution)/shard_map/ppermute | solution.py:19
  116.0 12.1 %collective-permute-start.12 = (f32[8,1,32,128]{3,0,2,1:T(8,128)S(1)}, f32[8,1,32,128]{3,0,2,1:T(8,128)S(1)}, u32[]{:S(2)}, u32[]{:S(2)}) collective-permute-start(f32[8,1,32,128]{3,0,2,1:T(8,128)S(1)} %get-tuple-element.56), channel_id=1, source_target_pairs={{4,0},{8,4},{12,8},{16,12},{20,16},{24,20},{28,24},{5,1},{9,5},{13... | collective-permute-start | bytes 393224 | tf_op jit(solution)/shard_map/ppermute | solution.py:20
  117.4 11.1 %collective-permute-start.31 = (f32[8,8,1,128]{3,0,2,1:T(8,128)S(1)}, f32[8,8,1,128]{3,0,2,1:T(8,128)S(1)}, u32[]{:S(2)}, u32[]{:S(2)}) collective-permute-start(f32[8,8,1,128]{3,0,2,1:T(8,128)S(1)} %get-tuple-element.42), channel_id=1, source_target_pairs={{0,1},{1,2},{2,3},{4,5},{5,6},{6,7},{8,9},{9,10},{10,11},{12,13},{... | collective-permute-start | bytes 98312 | tf_op jit(solution)/shard_map/ppermute | solution.py:19
  133.7 22.0 %collective-permute-start.34 = (f32[16,8,1,128]{3,0,2,1:T(8,128)S(1)}, f32[16,8,1,128]{3,0,2,1:T(8,128)S(1)}, u32[]{:S(2)}, u32[]{:S(2)}) collective-permute-start(f32[16,8,1,128]{3,0,2,1:T(8,128)S(1)} %get-tuple-element.27), channel_id=1, source_target_pairs={{1,0},{2,1},{3,2},{5,4},{6,5},{7,6},{9,8},{10,9},{11,10},{13,12},{... | collective-permute-start | bytes 196616 | tf_op jit(solution)/shard_map/ppermute | solution.py:20
  135.0 20.8 %collective-permute-start.35 = (f32[16,8,1,128]{3,0,2,1:T(8,128)S(1)}, f32[16,8,1,128]{3,0,2,1:T(8,128)S(1)}, u32[]{:S(2)}, u32[]{:S(2)}) collective-permute-start(f32[16,8,1,128]{3,0,2,1:T(8,128)S(1)} %get-tuple-element.28), channel_id=1, source_target_pairs={{0,1},{1,2},{2,3},{4,5},{5,6},{6,7},{8,9},{9,10},{10,11},{12,13},{... | collective-permute-start | bytes 196616 | tf_op jit(solution)/shard_map/ppermute | solution.py:19
  144.7 10.7 %collective-permute-start.32 = (f32[16,1,32,128]{3,0,2,1:T(8,128)S(1)}, f32[16,1,32,128]{3,0,2,1:T(8,128)S(1)}, u32[]{:S(2)}, u32[]{:S(2)}) collective-permute-start(f32[16,1,32,128]{3,0,2,1:T(8,128)S(1)} %get-tuple-element.30), channel_id=1, source_target_pairs={{4,0},{8,4},{12,8},{16,12},{20,16},{24,20},{28,24},{5,1},{9,5},{13... | collective-permute-start | bytes 786440 | tf_op jit(solution)/shard_map/ppermute | solution.py:20
  (20 other events, 150.8 us)
